TPU v7x, 512 devices: a whole 4x4x16 slice. The times are simulated.
512 devices in a mesh: rep: 32 (over z, core), row: 4 (over x), col: 4 (over y).
Axes of the slice: x: 4, y: 4, z: 16, core: 2. Of those that a mesh axis runs over, the one named last changes fastest.
Arguments:
- coordinates: bfloat16 [128, 32, 3, 128], P('rep')
- resample: int32 [32, 22], P('rep'), may hold values from 0 to 127, as said below
- block_slot: int32 [128], replicated, may hold values from 0 to 127, as said below
- lag_time: int32 [32], P('rep'), may hold values from 1 to 8
- atom_pairs: int32 [2, 4096], replicated, may hold values from 0 to 127, as said below
Outputs:
- instant_cov: bfloat16 [32, 4096, 4096], P('rep', 'row', 'col')
- lagged_cov: bfloat16 [32, 4096, 4096], P('rep', 'row', 'col')
Inputs may be any that keep to these rules, and one draw needn't show every extreme that they name: `resample`: the owner of a block is block_slot // 4. In each replicate at most 2 draws have one owner, and some owner has exactly 2; a block may be drawn more than once. `block_slot`: each slot holds exactly one block. `atom_pairs`: the two atoms of a feature differ, and no unordered pair of atoms appears twice.
All inputs are finite; a program needn't handle non-finite values.
Results may differ from a plain program's by a relative error of at most 0.0073.
Values may be sent and summed in bfloat16 or wider, within the bound.
No kernel may reach another device: no remote copies, remote signals or barrier semaphores. Data moves between devices by JAX's collectives and lax.ppermute only.
A program may use at most 64 MiB of HBM per device.

v0:
```python
import jax
import jax.numpy as jnp
from jax import lax
from jax.sharding import PartitionSpec as P

F = 4096
ATOMS = 128
BLOCK_LEN = 32
DRAWS = 22


def slot_lookup(lists, slot_table):
    matches = lists[..., None] == jnp.arange(slot_table.shape[0], dtype=jnp.int32)
    return jnp.sum(jnp.where(matches, slot_table, 0), axis=-1)


def owner_rank(lists, slot_table, blk_count):
    slots = slot_lookup(lists, slot_table)
    owner_ids = slots // blk_count
    local_ids = slots % blk_count
    draw_ids = jnp.arange(lists.shape[-1], dtype=jnp.int32)
    before = (owner_ids[..., :, None] == owner_ids[..., None, :]) & (
        draw_ids[None, :] < draw_ids[:, None]
    )
    ranks = jnp.sum(before.astype(jnp.int32), axis=-1)
    return (owner_ids, local_ids, ranks)


def pack_requests(resample, block_slot, local_data, capacity):
    every_list = lax.all_gather(resample, "rep", axis=0, tiled=True)
    blk_count = local_data.shape[0]
    owners_all, local_all, ranks_all = owner_rank(every_list, block_slot, blk_count)
    myself = lax.axis_index("rep")
    wanted = (owners_all == myself)[:, :, None] & (
        ranks_all[:, :, None] == jnp.arange(capacity, dtype=jnp.int32)
    )
    picked = local_all[:, :, None] == jnp.arange(blk_count, dtype=jnp.int32)
    selector = jnp.einsum(
        "rdc,rdk->rck", wanted.astype(jnp.float32), picked.astype(jnp.float32)
    ).astype(jnp.bfloat16)
    return jnp.einsum(
        "rck,kx->rcx", selector, local_data, preferred_element_type=jnp.float32
    ).astype(jnp.bfloat16)


def unpack_blocks(received, resample, block_slot, blk_count, capacity):
    owner_ids, local_ids, ranks = owner_rank(resample[0], block_slot, blk_count)
    rows_wanted = owner_ids * capacity + ranks
    flat = received.reshape(-1, received.shape[-1])
    return jnp.take(flat, rows_wanted, axis=0)


def tile_features(chosen, atom_pairs, first_feature, width, shift):
    first_atoms = lax.dynamic_slice_in_dim(atom_pairs[0], first_feature, width)
    second_atoms = lax.dynamic_slice_in_dim(atom_pairs[1], first_feature, width)
    atom_ids = jnp.arange(chosen.shape[-1], dtype=jnp.int32)[:, None]
    signed = (
        (atom_ids == first_atoms[None, :]).astype(jnp.float32)
        - (atom_ids == second_atoms[None, :]).astype(jnp.float32)
    ).astype(jnp.bfloat16)
    flat = chosen.reshape(-1, chosen.shape[-1])
    difference = jnp.dot(flat, signed, preferred_element_type=jnp.float32).reshape(
        DRAWS, BLOCK_LEN, 3, width
    )
    squared = (
        difference[:, :, 0] * difference[:, :, 0]
        + difference[:, :, 1] * difference[:, :, 1]
        + difference[:, :, 2] * difference[:, :, 2]
    )
    features = jnp.sqrt(squared).astype(jnp.bfloat16)
    doubled = jnp.concatenate([features, features], axis=1)
    shifted = lax.dynamic_slice_in_dim(doubled, shift, BLOCK_LEN, axis=1)
    valid_rows = (jnp.arange(BLOCK_LEN, dtype=jnp.int32) < BLOCK_LEN - shift)[None, :, None]
    pair_count = (2 * DRAWS * (BLOCK_LEN - shift)).astype(jnp.float32)
    earlier = jnp.where(valid_rows, features.astype(jnp.float32), 0.0)
    later = jnp.where(valid_rows, shifted.astype(jnp.float32), 0.0)
    feature_mean = (jnp.sum(earlier, axis=(0, 1)) + jnp.sum(later, axis=(0, 1))) / pair_count
    zero_lag = (
        jnp.where(valid_rows, earlier - feature_mean, 0.0).astype(jnp.bfloat16).reshape(-1, width)
    )
    lagged = (
        jnp.where(valid_rows, later - feature_mean, 0.0).astype(jnp.bfloat16).reshape(-1, width)
    )
    return (zero_lag, lagged, pair_count)


def shards(coordinates, resample, block_slot, lag_time, atom_pairs):
    rep_total = lax.axis_size("rep")
    per_owner = (DRAWS + rep_total - 1) // rep_total
    capacity = max(2, per_owner + per_owner // 2)
    blk_count = coordinates.shape[0]
    outgoing = pack_requests(resample, block_slot, coordinates.reshape(blk_count, -1), capacity)
    received = lax.all_to_all(outgoing, "rep", split_axis=0, concat_axis=0, tiled=True)
    chosen = unpack_blocks(received, resample, block_slot, blk_count, capacity).reshape(
        DRAWS, BLOCK_LEN, 3, ATOMS
    )
    width = F // lax.axis_size("row")
    shift = lag_time[0]
    zero_row, lag_row, pair_count = tile_features(
        chosen, atom_pairs, lax.axis_index("row") * width, width, shift
    )
    row_stack = jnp.concatenate([zero_row, lag_row], axis=0)
    zero_col, lag_col, unused_count = tile_features(
        chosen, atom_pairs, lax.axis_index("col") * width, width, shift
    )
    col_stack = jnp.concatenate([zero_col, lag_col], axis=0)
    half_rows = col_stack.shape[0] // 2
    mirrored = jnp.concatenate([col_stack[half_rows:], col_stack[:half_rows]], axis=0)
    instant = (
        jnp.einsum("na,nb->ab", row_stack, col_stack, preferred_element_type=jnp.float32)
        / pair_count
    )
    crossed = (
        jnp.einsum("na,nb->ab", row_stack, mirrored, preferred_element_type=jnp.float32)
        / pair_count
    )
    return (instant[None].astype(jnp.bfloat16), crossed[None].astype(jnp.bfloat16))


def solution(mesh):
    return jax.shard_map(
        shards,
        mesh=mesh,
        in_specs=(P("rep", None, None, None), P("rep", None), P(), P("rep"), P()),
        out_specs=(P("rep", "row", "col"), P("rep", "row", "col")),
        check_vma=False,
    )
```

profile of v0, /device:TPU:1, one launch (start us, length us, event | category | flops | bytes accessed | tf_op | source)
XLA Modules:
  0.0 158.3 jit_solution(3388728040057878747)
XLA Ops:
  0.7 37.5 %all-gather = s32[32,1,22]{2,1,0:T(1,128)S(1)} all-gather(s32[1,1,22]{2,1,0:T(1,128)} %bitcast.64), channel_id=1, replica_groups=mesh['rep'=32,'row'=4,'col'=4] {'rep'}, dimensions={0}, use_global_device_ids=true | all-gather | bytes 2904 | tf_op jit(solution)/shard_map/all_gather | solution.py:30
  38.2 0.1 copy.26
  38.3 1.2 select_reduce_fusion.2
  39.5 0.2 convert_reduce_fusion
  39.7 0.1 copy.28
  39.8 0.1 copy.27
  39.9 0.1 copy.29
  40.0 1.0 copy.30
  40.9 0.1 reshape.274
  41.0 0.2 convolution_convert_fusion.1
  41.2 0.5 convolution_convert_fusion
  41.8 2.8 %copy.32 = bf16[32,2,12288]{2,1,0:T(2,128)(2,1)} copy(bf16[32,2,12288]{2,0,1:T(8,128)(2,1)S(1)} %convolution_convert_fusion) | data formatting | bytes 3145728 | tf_op jit(solution)/shard_map/convert_element_type | solution.py:43
  44.5 7.0 %all-to-all-start = ((bf16[32,2,12288]{2,1,0:T(2,128)(2,1)}), bf16[32,2,12288]{2,1,0:T(2,128)(2,1)S(1)}, u32[]{:S(2)}, u32[]{:S(2)}) async-start(bf16[32,2,12288]{2,1,0:T(2,128)(2,1)} %copy.32), calls=%async_computation | async-start | bytes 3145728 | tf_op jit(solution)/shard_map/all_to_all | solution.py:93
  52.2 0.1 broadcast_in_dim.106
  52.3 0.2 select_reduce_fusion.3
  52.5 0.2 convert_reduce_fusion.1
  52.8 76.7 %all-to-all-done = bf16[32,2,12288]{2,1,0:T(2,128)(2,1)S(1)} async-done(((bf16[32,2,12288]{2,1,0:T(2,128)(2,1)}), bf16[32,2,12288]{2,1,0:T(2,128)(2,1)S(1)}, u32[]{:S(2)}, u32[]{:S(2)}) %all-to-all-start) | async-done | bytes 1572896 | tf_op jit(solution)/shard_map/all_to_all | solution.py:93
  129.5 0.6 reshape.259
  130.1 0.9 gather_fusion
  131.0 0.8 gather.7
  131.8 0.4 broadcast_select_fusion
  132.2 1.3 fusion.32
  133.5 1.2 fusion.56
  134.8 1.2 fusion.2
  136.0 1.3 fusion.34
  137.3 1.2 fusion.57
  138.5 1.2 fusion.6
  139.7 5.3 %fusion.23 = (f32[1024]{0:T(1024)S(1)}, f32[1024]{0:T(1024)S(1)}, f32[1024]{0:T(1024)S(1)}, f32[1024]{0:T(1024)S(1)}) fusion(pred[32]{0:T(512)(128)(4,1)S(1)} %iota_compare_fusion.9, s32[]{:T(128)S(6)} %select_n.137, bf16[22,32,1024]{2,1,0:T(8,128)(2,1)S(1)} %fusion.57, bf16[22,32,1024]{2,1,0:T(8,128)(2,1)S(1)} %fusion.56, ...), kind=kLoop, calls=%fused_computation.45 | loop fusion | flops 21622784 | bytes 20201508 | tf_op jit(solution)/shard_map/reduce_sum | solution.py:77
  145.0 2.6 %select_convert_fusion.1 = (bf16[22,32,1024]{2,1,0:T(8,128)(2,1)S(1)}, bf16[22,32,1024]{2,1,0:T(8,128)(2,1)S(1)}) fusion(f32[1024]{0:T(1024)S(1)} %get-tuple-element.19, pred[32]{0:T(512)(128)(4,1)S(1)} %iota_compare_fusion.9, s32[]{:T(128)S(6)} %select_n.137, bf16[22,32,1024]{2,1,0:T(8,128)(2,1)S(1)} %fusion.57, f32[1024]{0:T(1024)S(1)} %get-tuple-element.18, ...), kind=kLoop, calls=%fused_computation.43 | loop fusion | flops 11534336 | bytes 5775396 | tf_op jit(solution)/shard_map/convert_element_type | solution.py:82
  147.6 1.4 fusion.21
  149.0 4.7 %fusion.25 = bf16[1,1024,1024]{2,1,0:T(8,128)(2,1)} fusion(f32[]{:T(128)S(6)} %convert_element_type.94, bf16[704,1024]{1,0:T(8,128)(2,1)S(1)} %get-tuple-element.15, bf16[704,1024]{1,0:T(8,128)(2,1)S(1)} %bitcast.57, bf16[704,1024]{1,0:T(8,128)(2,1)S(1)} %bitcast.55, bf16[704,1024]{1,0:T(8,128)(2,1)S(1)} %get-tuple-element.14), kind=kOutput, calls=%fused_computation.48 | convolution fusion | flops 2966421504 | bytes 7864324 | tf_op jit(solution)/shard_map/na,nb->ab/dot_general | solution.py:114
  153.7 4.6 %fusion.24 = bf16[1,1024,1024]{2,1,0:T(8,128)(2,1)} fusion(f32[]{:T(128)S(6)} %convert_element_type.94, bf16[704,1024]{1,0:T(8,128)(2,1)S(1)} %bitcast.58, bf16[704,1024]{1,0:T(8,128)(2,1)S(1)} %get-tuple-element.15, bf16[704,1024]{1,0:T(8,128)(2,1)S(1)} %bitcast.56, bf16[704,1024]{1,0:T(8,128)(2,1)S(1)} %get-tuple-element.14), kind=kOutput, calls=%fused_computation.47 | convolution fusion | flops 2966421504 | bytes 7864324 | tf_op jit(solution)/shard_map/na,nb->ab/dot_general | solution.py:110
  (19 shorter events, 0.2 us)
Async XLA Ops:
  41.7 10.6 %copy-start.1 = (s32[128]{0:T(128)S(1)}, s32[128]{0:T(128)}, u32[]{:S(2)}) copy-start(s32[128]{0:T(128)} %param.7) | copy-start | bytes 1540
  41.8 10.6 %copy-start.2 = (s32[1,22]{1,0:T(1,128)S(1)}, s32[1,22]{1,0:T(1,128)}, u32[]{:S(2)}) copy-start(s32[1,22]{1,0:T(1,128)} %param.6) | copy-start | bytes 268
  41.8 11.0 %copy-start = (s32[2,4096]{1,0:T(2,128)S(1)}, s32[2,4096]{1,0:T(2,128)}, u32[]{:S(2)}) copy-start(s32[2,4096]{1,0:T(2,128)} %param.9) | copy-start | bytes 98308
  44.5 85.0 %all-to-all-start = ((bf16[32,2,12288]{2,1,0:T(2,128)(2,1)}), bf16[32,2,12288]{2,1,0:T(2,128)(2,1)S(1)}, u32[]{:S(2)}, u32[]{:S(2)}) async-start(bf16[32,2,12288]{2,1,0:T(2,128)(2,1)} %copy.32), calls=%async_computation | async-start | bytes 3145728 | tf_op jit(solution)/shard_map/all_to_all | solution.py:93
where the time goes:
time: 159 us; the launch traced here: 158 us
  waiting for transfers between devices  76.7 us (48%)
  blocking collectives  37.5 us (24%)
  other arithmetic  16.4 us (10%)
  matrix products  12.6 us (8%)
  starting transfers between devices  6.98 us (4%)
  local copies, waits for them, and re-layouts  6.61 us (4%)
    all_to_all x1, waiting for transfers between devices, shards(): lax.all_to_all(outgoing, 'rep', split_axis=0, concat_axis=0, tiled=True)  76.7 us
    all_gather x1, blocking collectives, pack_requests(): every_list = lax.all_gather(resample, 'rep', axis=0, tiled=True)  37.5 us
    all_to_all x1, starting transfers between devices, shards(): lax.all_to_all(outgoing, 'rep', split_axis=0, concat_axis=0, tiled=True)  6.98 us
    reduce_sum x1, other arithmetic, tile_features(): jnp.sum(later, axis=(0, 1))  5.29 us
    dot_general x1, matrix products, shards(): jnp.einsum('na,nb->ab', row_stack, mirrored, preferred_element_type=jnp.f...  4.67 us
    dot_general x1, matrix products, shards(): jnp.einsum('na,nb->ab', row_stack, col_stack, preferred_element_type=jnp....  4.65 us
  transfers between devices with their start and end apart: 1, of which 1 were waited for; matrix products, arithmetic and copies ran while one was open for 0% of the time, Pallas kernels for 0%

commit v1 on v0

--- a/solution.py
+++ b/solution.py
@@ -9,45 +9,21 @@
 DRAWS = 22
 
 
-def slot_lookup(lists, slot_table):
-    matches = lists[..., None] == jnp.arange(slot_table.shape[0], dtype=jnp.int32)
-    return jnp.sum(jnp.where(matches, slot_table, 0), axis=-1)
-
-
-def owner_rank(lists, slot_table, blk_count):
-    slots = slot_lookup(lists, slot_table)
-    owner_ids = slots // blk_count
-    local_ids = slots % blk_count
-    draw_ids = jnp.arange(lists.shape[-1], dtype=jnp.int32)
-    before = (owner_ids[..., :, None] == owner_ids[..., None, :]) & (
-        draw_ids[None, :] < draw_ids[:, None]
-    )
-    ranks = jnp.sum(before.astype(jnp.int32), axis=-1)
-    return (owner_ids, local_ids, ranks)
-
-
-def pack_requests(resample, block_slot, local_data, capacity):
-    every_list = lax.all_gather(resample, "rep", axis=0, tiled=True)
-    blk_count = local_data.shape[0]
-    owners_all, local_all, ranks_all = owner_rank(every_list, block_slot, blk_count)
-    myself = lax.axis_index("rep")
-    wanted = (owners_all == myself)[:, :, None] & (
-        ranks_all[:, :, None] == jnp.arange(capacity, dtype=jnp.int32)
-    )
-    picked = local_all[:, :, None] == jnp.arange(blk_count, dtype=jnp.int32)
-    selector = jnp.einsum(
-        "rdc,rdk->rck", wanted.astype(jnp.float32), picked.astype(jnp.float32)
-    ).astype(jnp.bfloat16)
-    return jnp.einsum(
-        "rck,kx->rcx", selector, local_data, preferred_element_type=jnp.float32
-    ).astype(jnp.bfloat16)
-
-
-def unpack_blocks(received, resample, block_slot, blk_count, capacity):
-    owner_ids, local_ids, ranks = owner_rank(resample[0], block_slot, blk_count)
-    rows_wanted = owner_ids * capacity + ranks
-    flat = received.reshape(-1, received.shape[-1])
-    return jnp.take(flat, rows_wanted, axis=0)
+def gather_blocks(coordinates, resample, block_slot):
+    groups = lax.axis_size("row") * lax.axis_size("col")
+    if BLOCK_LEN % groups:
+        groups = 1
+    frames = BLOCK_LEN // groups
+    member = lax.axis_index("row") * lax.axis_size("col") + lax.axis_index("col")
+    if groups == 1:
+        member = 0
+    piece = lax.dynamic_slice_in_dim(coordinates, member * frames, frames, axis=1)
+    every = lax.all_gather(piece, "rep", axis=0, tiled=True)
+    slots = jnp.take(block_slot, resample[0], axis=0)
+    picked = jnp.take(every, slots, axis=0)
+    if groups == 1:
+        return picked
+    return lax.all_gather(picked, ("row", "col"), axis=1, tiled=True)
 
 
 def tile_features(chosen, atom_pairs, first_feature, width, shift):
@@ -85,15 +61,7 @@
 
 
 def shards(coordinates, resample, block_slot, lag_time, atom_pairs):
-    rep_total = lax.axis_size("rep")
-    per_owner = (DRAWS + rep_total - 1) // rep_total
-    capacity = max(2, per_owner + per_owner // 2)
-    blk_count = coordinates.shape[0]
-    outgoing = pack_requests(resample, block_slot, coordinates.reshape(blk_count, -1), capacity)
-    received = lax.all_to_all(outgoing, "rep", split_axis=0, concat_axis=0, tiled=True)
-    chosen = unpack_blocks(received, resample, block_slot, blk_count, capacity).reshape(
-        DRAWS, BLOCK_LEN, 3, ATOMS
-    )
+    chosen = gather_blocks(coordinates, resample, block_slot)
     width = F // lax.axis_size("row")
     shift = lag_time[0]
     zero_row, lag_row, pair_count = tile_features(

time: 159 us -> 109 us (0.69)
  the two profiles are of different devices: /device:TPU:1 before, /device:TPU:2 now
where the time goes in v1:
time: 109 us
  blocking collectives  60.9 us (56%)
  other arithmetic  27.3 us (25%)
  matrix products  11.9 us (11%)
  local copies, waits for them, and re-layouts  7.29 us (7%)
  between operations  1.45 us (1%)
    all_gather x1, blocking collectives, gather_blocks(): every = lax.all_gather(piece, 'rep', axis=0, tiled=True)  36.8 us
    all_gather x1, blocking collectives, gather_blocks(): return lax.all_gather(picked, ('row', 'col'), axis=1, tiled=True)  24.1 us
    reduce_sum x1, other arithmetic, tile_features(): jnp.sum(later, axis=(0, 1))  8.72 us
    another operation x2, other arithmetic  8.31 us
    dot_general x1, matrix products, shards(): jnp.einsum('na,nb->ab', row_stack, mirrored, preferred_element_type=jnp.f...  4.67 us
    dot_general x1, matrix products, shards(): jnp.einsum('na,nb->ab', row_stack, col_stack, preferred_element_type=jnp....  4.64 us
    unnamed x8, local copies, waits for them, and re-layouts  4.3 us
    convert_element_type x1, other arithmetic, tile_features(): jnp.where(valid_rows, earlier - feature_mean, 0.0).astype(jnp.bfloat16)  3.09 us

profile of v1, /device:TPU:2, one launch (start us, length us, event | category | flops | bytes accessed | tf_op | source)
XLA Modules:
  0.0 108.9 jit_solution(13588767077936588273)
XLA Ops:
  0.6 0.0 copy-start
  0.7 0.9 fusion.48
  1.6 0.0 copy-done
  1.6 36.8 %all_gather.6 = bf16[128,2,3,128]{3,1,2,0:T(2,128)(2,1)S(1)} all-gather(bf16[4,2,3,128]{3,1,2,0:T(2,128)(2,1)S(1)} %constant_dynamic-slice_fusion.4), channel_id=1, replica_groups=mesh['rep'=32,'row'=4,'col'=4] {'rep'}, dimensions={0}, use_global_device_ids=true | all-gather | bytes 202752 | tf_op jit(solution)/shard_map/all_gather | solution.py:21
  38.4 0.7 fusion.47
  39.0 1.4 %gather_fusion = s32[22]{0:T(128)S(1)} fusion(s32[128]{0:T(128)} %param.7, s32[1024]{0:T(1024)S(1)} %pad_clamp_fusion.1), kind=kCustom, calls=%fused_computation | custom fusion | bytes 264 | tf_op jit(solution)/shard_map/jit(_take)/gather | solution.py:22
  40.4 0.7 fusion.44
  41.1 0.6 gather_fusion.1
  41.7 0.7 compare_and_fusion
  42.4 0.1 broadcast_select_fusion
  42.5 24.1 %all_gather.7 = bf16[22,32,3,128]{3,0,2,1:T(8,128)(2,1)S(1)} all-gather(bf16[22,2,3,128]{3,0,2,1:T(8,128)(2,1)S(1)} %copy.13), channel_id=1, replica_groups=mesh['rep'=32,'row'=4,'col'=4] {'row','col'}, dimensions={1}, use_global_device_ids=true | all-gather | bytes 574464 | tf_op jit(solution)/shard_map/all_gather | solution.py:26
  66.6 1.3 %fusion.32 = f32[22,32,3,1024]{3,1,0,2:T(8,128)S(1)} fusion(bf16[22,32,3,128]{3,0,2,1:T(8,128)(2,1)S(1)} %all_gather.7, s32[1024]{0:T(1024)S(1)} %bitcast.60, s32[1024]{0:T(1024)S(1)} %bitcast.58), kind=kOutput, calls=%fused_computation.51 | convolution fusion | flops 554434560 | bytes 9199616 | tf_op jit(solution)/shard_map/dot_general | solution.py:38
  68.0 0.0 copy-start.1
  68.0 1.2 %fusion.49 = bf16[22,32,1024]{2,1,0:T(8,128)(2,1)S(1)} fusion(f32[22,32,3,1024]{3,1,0,2:T(8,128)S(1)} %fusion.32), kind=kLoop, calls=%fused_computation.90 | loop fusion | flops 4325376 | bytes 10092544 | tf_op jit(solution)/shard_map/sqrt | solution.py:46
  69.2 2.1 %copy-done.1 = f32[22,32,3,1024]{3,1,0,2:T(8,128)} copy-done((f32[22,32,3,1024]{3,1,0,2:T(8,128)}, f32[22,32,3,1024]{3,1,0,2:T(8,128)S(1)}, u32[]{:S(2)}) %copy-start.1) | copy-done | bytes 8650776
  71.3 1.3 %fusion.34 = f32[22,32,3,1024]{3,1,2,0:T(8,128)S(1)} fusion(bf16[22,32,3,128]{3,0,2,1:T(8,128)(2,1)S(1)} %all_gather.7, s32[1024]{0:T(1024)S(1)} %bitcast.59, s32[1024]{0:T(1024)S(1)} %bitcast.57), kind=kOutput, calls=%fused_computation.53 | convolution fusion | flops 554434560 | bytes 9199616 | tf_op jit(solution)/shard_map/dot_general | solution.py:38
  72.6 0.0 copy-start.2
  72.6 1.2 %fusion.50 = bf16[22,32,1024]{2,1,0:T(8,128)(2,1)S(1)} fusion(f32[22,32,3,1024]{3,1,2,0:T(8,128)S(1)} %fusion.34), kind=kLoop, calls=%fused_computation.91 | loop fusion | flops 4325376 | bytes 10092544 | tf_op jit(solution)/shard_map/sqrt | solution.py:46
  73.9 2.1 %copy-done.2 = f32[22,32,3,1024]{3,1,2,0:T(8,128)} copy-done((f32[22,32,3,1024]{3,1,2,0:T(8,128)}, f32[22,32,3,1024]{3,1,2,0:T(8,128)S(1)}, u32[]{:S(2)}) %copy-start.2) | copy-done | bytes 8650776
  76.6 8.7 %fusion.23 = (f32[1024]{0:T(1024)S(1)}, f32[1024]{0:T(1024)S(1)}, f32[1024]{0:T(1024)S(1)}, f32[1024]{0:T(1024)S(1)}) fusion(pred[32]{0:T(512)(128)(4,1)S(1)} %iota_compare_fusion.4, s32[]{:T(128)S(6)} %select_n.115, bf16[22,32,1024]{2,1,0:T(8,128)(2,1)S(1)} %fusion.50, bf16[22,32,1024]{2,1,0:T(8,128)(2,1)S(1)} %fusion.49, f32[22,32,3,1024]{3,1,0,2:T(8,128)} %copy-done.1, ...), kind=kLoop, calls=%fused_computation.45 | loop fusion | flops 21622784 | bytes 20201508 | tf_op jit(solution)/shard_map/reduce_sum | solution.py:53
  85.4 0.0 copy-start.3
  85.4 6.0 %fusion.2 = bf16[22,32,1,1024]{3,1,0,2:T(8,128)(2,1)} fusion(f32[22,32,3,1024]{3,1,0,2:T(8,128)} %copy-done.1), kind=kLoop, calls=%fused_computation.7 | loop fusion | flops 4325376 | bytes 10092544 | tf_op jit(solution)/shard_map/convert.1
  91.4 0.1 copy-done.3
  91.5 2.3 %fusion.6 = bf16[22,32,1,1024]{3,1,2,0:T(8,128)(2,1)} fusion(f32[22,32,3,1024]{3,1,2,0:T(8,128)S(1)} %copy-done.3), kind=kLoop, calls=%fused_computation.14 | loop fusion | flops 4325376 | bytes 10092544 | tf_op jit(solution)/shard_map/convert.3
  93.8 0.1 broadcast_in_dim.75
  93.9 3.1 %fusion.21 = (bf16[704,1024]{1,0:T(8,128)(2,1)S(1)}, bf16[704,1024]{1,0:T(8,128)(2,1)S(1)}) fusion(bf16[22,32,1,1024]{3,1,2,0:T(8,128)(2,1)} %fusion.6, f32[1024]{0:T(1024)S(1)} %get-tuple-element.17, pred[704]{0:T(1024)(128)(4,1)S(1)} %broadcast_in_dim.75, f32[1024]{0:T(1024)S(1)} %get-tuple-element.16, bf16[22,32,1,1024]{3,1,0,2:T(8,128)(2,1)} %fusion.2), kind=kLoop, calls=%fused_computation.38 | loop fusion | flops 7208960 | bytes 5776064 | tf_op jit(solution)/shard_map/convert_element_type | solution.py:55
  97.0 2.6 %select_convert_fusion.1 = (bf16[22,32,1024]{2,1,0:T(8,128)(2,1)S(1)}, bf16[22,32,1024]{2,1,0:T(8,128)(2,1)S(1)}) fusion(f32[1024]{0:T(1024)S(1)} %get-tuple-element.17, pred[32]{0:T(512)(128)(4,1)S(1)} %iota_compare_fusion.4, s32[]{:T(128)S(6)} %select_n.115, bf16[22,32,1024]{2,1,0:T(8,128)(2,1)S(1)} %fusion.50, f32[1024]{0:T(1024)S(1)} %get-tuple-element.16, ...), kind=kLoop, calls=%fused_computation.43 | loop fusion | flops 11534336 | bytes 5775396 | tf_op jit(solution)/shard_map/convert_element_type | solution.py:58
  99.6 4.7 %fusion.25 = bf16[1,1024,1024]{2,1,0:T(8,128)(2,1)} fusion(f32[]{:T(128)S(6)} %convert_element_type.76, bf16[704,1024]{1,0:T(8,128)(2,1)S(1)} %get-tuple-element.13, bf16[704,1024]{1,0:T(8,128)(2,1)S(1)} %bitcast.55, bf16[704,1024]{1,0:T(8,128)(2,1)S(1)} %bitcast.53, bf16[704,1024]{1,0:T(8,128)(2,1)S(1)} %get-tuple-element.12), kind=kOutput, calls=%fused_computation.48 | convolution fusion | flops 2966421504 | bytes 7864324 | tf_op jit(solution)/shard_map/na,nb->ab/dot_general | solution.py:82
  104.3 4.6 %fusion.24 = bf16[1,1024,1024]{2,1,0:T(8,128)(2,1)} fusion(f32[]{:T(128)S(6)} %convert_element_type.76, bf16[704,1024]{1,0:T(8,128)(2,1)S(1)} %bitcast.56, bf16[704,1024]{1,0:T(8,128)(2,1)S(1)} %get-tuple-element.13, bf16[704,1024]{1,0:T(8,128)(2,1)S(1)} %bitcast.54, bf16[704,1024]{1,0:T(8,128)(2,1)S(1)} %get-tuple-element.12), kind=kOutput, calls=%fused_computation.47 | convolution fusion | flops 2966421504 | bytes 7864324 | tf_op jit(solution)/shard_map/na,nb->ab/dot_general | solution.py:78
  (9 shorter events, 0.1 us)
Async XLA Ops:
  0.6 0.9 copy-start
  68.0 3.3 %copy-start.1 = (f32[22,32,3,1024]{3,1,0,2:T(8,128)}, f32[22,32,3,1024]{3,1,0,2:T(8,128)S(1)}, u32[]{:S(2)}) copy-start(f32[22,32,3,1024]{3,1,0,2:T(8,128)S(1)} %fusion.32) | copy-start | bytes 25952260
  72.6 3.3 %copy-start.2 = (f32[22,32,3,1024]{3,1,2,0:T(8,128)}, f32[22,32,3,1024]{3,1,2,0:T(8,128)S(1)}, u32[]{:S(2)}) copy-start(f32[22,32,3,1024]{3,1,2,0:T(8,128)S(1)} %fusion.34) | copy-start | bytes 25952260
  85.4 6.1 %copy-start.3 = (f32[22,32,3,1024]{3,1,2,0:T(8,128)S(1)}, f32[22,32,3,1024]{3,1,2,0:T(8,128)}, u32[]{:S(2)}) copy-start(f32[22,32,3,1024]{3,1,2,0:T(8,128)} %copy-done.2) | copy-start | bytes 25952260

commit v2 on v1

v2 whole, which is shorter than its diff:
```python
import functools

import jax
import jax.numpy as jnp
from jax import lax
from jax.experimental import pallas as pl
from jax.experimental.pallas import tpu as pltpu
from jax.sharding import PartitionSpec as P

F = 4096
ATOMS = 128
BLOCK_LEN = 32
DRAWS = 22
TILE = 256


def gather_blocks(coordinates, resample, block_slot):
    groups = lax.axis_size("row") * lax.axis_size("col")
    if BLOCK_LEN % groups:
        groups = 1
    frames = BLOCK_LEN // groups
    member = lax.axis_index("row") * lax.axis_size("col") + lax.axis_index("col")
    if groups == 1:
        member = 0
    piece = lax.dynamic_slice_in_dim(coordinates, member * frames, frames, axis=1)
    reps = lax.axis_size("rep")
    spread = jnp.broadcast_to(piece[None], (reps,) + piece.shape)
    every = lax.all_to_all(spread, "rep", 0, 0, tiled=True)
    every = every.reshape((-1,) + piece.shape[1:])
    slots = jnp.take(block_slot, resample[0], axis=0)
    picked = jnp.take(every, slots, axis=0)
    if groups == 1:
        return picked
    spread = jnp.broadcast_to(picked[None], (groups,) + picked.shape)
    parts = lax.all_to_all(spread, ("row", "col"), 0, 0, tiled=True)
    return jnp.swapaxes(parts, 0, 1).reshape(DRAWS, BLOCK_LEN, 3, ATOMS)


def centered_kernel(lag_ref, x_ref, xs_ref, s_ref, out_ref):
    lag = lag_ref[0]
    signed = s_ref[...]

    def distances(ref):
        total = None
        for c in range(3):
            d = jnp.dot(ref[c], signed, preferred_element_type=jnp.float32)
            total = d * d if total is None else total + d * d
        return jnp.sqrt(total).astype(jnp.bfloat16).astype(jnp.float32)

    earlier = distances(x_ref)
    later = distances(xs_ref)
    rows = lax.broadcasted_iota(jnp.int32, earlier.shape, 0)
    valid = (rows % BLOCK_LEN) < (BLOCK_LEN - lag)
    earlier = jnp.where(valid, earlier, 0.0)
    later = jnp.where(valid, later, 0.0)
    count = (2 * DRAWS * (BLOCK_LEN - lag)).astype(jnp.float32)
    mean = (
        jnp.sum(earlier, axis=0, keepdims=True) + jnp.sum(later, axis=0, keepdims=True)
    ) / count
    out_ref[0] = jnp.where(valid, earlier - mean, 0.0).astype(jnp.bfloat16)
    out_ref[1] = jnp.where(valid, later - mean, 0.0).astype(jnp.bfloat16)


def centered_pairs(lag, frames, shifted, signed):
    n = frames.shape[1]
    width = signed.shape[1]
    return pl.pallas_call(
        centered_kernel,
        grid=(width // TILE,),
        in_specs=[
            pl.BlockSpec(memory_space=pltpu.SMEM),
            pl.BlockSpec((3, n, ATOMS), lambda j: (0, 0, 0)),
            pl.BlockSpec((3, n, ATOMS), lambda j: (0, 0, 0)),
            pl.BlockSpec((ATOMS, TILE), lambda j: (0, j)),
        ],
        out_specs=pl.BlockSpec((2, n, TILE), lambda j: (0, 0, j)),
        out_shape=jax.ShapeDtypeStruct((2, n, width), jnp.bfloat16),
        cost_estimate=pl.CostEstimate(
            flops=2 * 2 * 3 * n * ATOMS * width,
            transcendentals=2 * n * width,
            bytes_accessed=2 * n * width * 2 + 2 * 3 * n * ATOMS * 2 + ATOMS * width * 2,
        ),
    )(lag, frames, shifted, signed)


def signed_pairs(atom_pairs, first_feature, width):
    first_atoms = lax.dynamic_slice_in_dim(atom_pairs[0], first_feature, width)
    second_atoms = lax.dynamic_slice_in_dim(atom_pairs[1], first_feature, width)
    atom_ids = jnp.arange(ATOMS, dtype=jnp.int32)[:, None]
    return (
        (atom_ids == first_atoms[None, :]).astype(jnp.float32)
        - (atom_ids == second_atoms[None, :]).astype(jnp.float32)
    ).astype(jnp.bfloat16)


def shards(coordinates, resample, block_slot, lag_time, atom_pairs):
    chosen = gather_blocks(coordinates, resample, block_slot)
    width = F // lax.axis_size("row")
    shift = lag_time[0]
    doubled = jnp.concatenate([chosen, chosen], axis=1)
    moved = lax.dynamic_slice_in_dim(doubled, shift, BLOCK_LEN, axis=1)
    frames = jnp.transpose(chosen, (2, 0, 1, 3)).reshape(3, DRAWS * BLOCK_LEN, ATOMS)
    shifted = jnp.transpose(moved, (2, 0, 1, 3)).reshape(3, DRAWS * BLOCK_LEN, ATOMS)
    row_signed = signed_pairs(atom_pairs, lax.axis_index("row") * width, width)
    col_signed = signed_pairs(atom_pairs, lax.axis_index("col") * width, width)
    row_stack = centered_pairs(lag_time, frames, shifted, row_signed)
    col_stack = centered_pairs(lag_time, frames, shifted, col_signed)
    pair_count = (2 * DRAWS * (BLOCK_LEN - shift)).astype(jnp.float32)
    rows = row_stack.reshape(-1, width)
    instant = (
        jnp.einsum("na,nb->ab", rows, col_stack.reshape(-1, width), preferred_element_type=jnp.float32)
        / pair_count
    )
    crossed = (
        jnp.einsum("na,nb->ab", rows, col_stack[::-1].reshape(-1, width), preferred_element_type=jnp.float32)
        / pair_count
    )
    return (instant[None].astype(jnp.bfloat16), crossed[None].astype(jnp.bfloat16))


def solution(mesh):
    return jax.shard_map(
        shards,
        mesh=mesh,
        in_specs=(P("rep", None, None, None), P("rep", None), P(), P("rep"), P()),
        out_specs=(P("rep", "row", "col"), P("rep", "row", "col")),
        check_vma=False,
    )
```

time: 109 us -> 85.9 us (0.79)
  the two profiles are of different devices: /device:TPU:2 before, /device:TPU:1 now
where the time goes in v2:
time: 85.9 us; the launch traced here: 84.7 us
  starting transfers between devices  23.5 us (27%)
  waiting for transfers between devices  21.4 us (25%)
  Pallas kernels  15.2 us (18%)
  matrix products  11.3 us (13%)
  local copies, waits for them, and re-layouts  7.71 us (9%)
  other arithmetic  4.16 us (5%)
  between operations  1.37 us (2%)
    all_to_all x1, starting transfers between devices, gather_blocks(): every = lax.all_to_all(spread, 'rep', 0, 0, tiled=True)  16.7 us
    pallas_call x2, Pallas kernels, centered_pairs(): pl.pallas_call(centered_kernel, grid=(width // TILE,), in_specs=[pl.Block...  15.2 us
    all_to_all x1, waiting for transfers between devices, gather_blocks(): every = lax.all_to_all(spread, 'rep', 0, 0, tiled=True)  14.4 us
    all_to_all x1, waiting for transfers between devices, gather_blocks(): parts = lax.all_to_all(spread, ('row', 'col'), 0, 0, tiled=True)  7.04 us
    all_to_all x1, starting transfers between devices, gather_blocks(): parts = lax.all_to_all(spread, ('row', 'col'), 0, 0, tiled=True)  6.75 us
    dot_general x1, matrix products, shards(): jnp.einsum('na,nb->ab', rows, col_stack[::-1].reshape(-1, width), preferr...  6.63 us
    dot_general x1, matrix products, shards(): jnp.einsum('na,nb->ab', rows, col_stack.reshape(-1, width), preferred_ele...  4.68 us
  transfers between devices with their start and end apart: 2, of which 2 were waited for; matrix products, arithmetic and copies ran while one was open for 7% of the time, Pallas kernels for 0%

profile of v2, /device:TPU:1, one launch (start us, length us, event | category | flops | bytes accessed | tf_op | source)
XLA Modules:
  0.0 84.7 jit_solution(16885947576168354076)
XLA Ops:
  0.6 0.0 copy-start
  0.7 0.9 %copy-done = bf16[4,32,3,128]{3,1,2,0:T(8,128)(2,1)S(1)} copy-done((bf16[4,32,3,128]{3,1,2,0:T(8,128)(2,1)S(1)}, bf16[4,32,3,128]{3,1,2,0:T(8,128)(2,1)}, u32[]{:S(2)}) %copy-start) | copy-done | bytes 98328
  1.5 0.8 broadcast_in_dim.17
  2.3 16.7 %all-to-all-start = ((bf16[32,4,2,3,128]{4,2,3,1,0:T(2,128)(2,1)}), bf16[32,4,2,3,128]{4,2,3,1,0:T(2,128)(2,1)S(1)}, u32[]{:S(2)}, u32[]{:S(2)}) async-start(bf16[32,4,2,3,128]{4,2,3,1,0:T(2,128)(2,1)} %broadcast_in_dim.17), calls=%async_computation | async-start | bytes 393216 | tf_op jit(solution)/shard_map/all_to_all | solution.py:28
  19.1 0.7 fusion.7
  19.8 1.4 %gather_fusion = s32[22]{0:T(128)S(1)} fusion(s32[128]{0:T(128)} %param.7, s32[1024]{0:T(1024)S(1)} %pad_clamp_fusion.1), kind=kCustom, calls=%fused_computation | custom fusion | bytes 264 | tf_op jit(solution)/shard_map/jit(_take)/gather | solution.py:30
  21.1 0.7 compare_and_fusion
  21.8 0.7 fusion.6
  22.5 0.9 %fusion.8 = (s32[1,4096]{1,0:T(1,128)S(1)}, s32[1,4096]{1,0:T(1,128)S(1)}) fusion(s32[2,4096]{1,0:T(2,128)} %param.9), kind=kLoop, calls=%fused_computation.35 | loop fusion | bytes 65536 | tf_op jit(solution)/shard_map/slice | solution.py:87
  23.3 14.4 %all-to-all-done = bf16[32,4,2,3,128]{4,2,3,1,0:T(2,128)(2,1)S(1)} async-done(((bf16[32,4,2,3,128]{4,2,3,1,0:T(2,128)(2,1)}), bf16[32,4,2,3,128]{4,2,3,1,0:T(2,128)(2,1)S(1)}, u32[]{:S(2)}, u32[]{:S(2)}) %all-to-all-start) | async-done | bytes 196640 | tf_op jit(solution)/shard_map/all_to_all | solution.py:28
  37.7 0.6 gather_fusion.1
  38.3 0.1 broadcast_select_fusion
  38.5 1.1 %broadcast_in_dim.19 = bf16[16,22,2,3,128]{4,2,1,3,0:T(2,128)(2,1)} broadcast(bf16[22,2,3,128]{3,1,0,2:T(2,128)(2,1)S(1)} %copy.10), dimensions={1,2,3,4} | broadcast | bytes 574464 | tf_op jit(solution)/shard_map/broadcast_in_dim | solution.py:34
  39.6 6.8 %all-to-all-start.1 = ((bf16[16,22,2,3,128]{4,2,1,3,0:T(2,128)(2,1)}), bf16[16,22,2,3,128]{4,2,1,3,0:T(2,128)(2,1)S(1)}, u32[]{:S(2)}, u32[]{:S(2)}) async-start(bf16[16,22,2,3,128]{4,2,1,3,0:T(2,128)(2,1)} %broadcast_in_dim.19), calls=%async_computation.1 | async-start | bytes 1081344 | tf_op jit(solution)/shard_map/all_to_all | solution.py:35
  47.0 0.8 subtract_convert_fusion.1.s_ref
  47.8 0.8 subtract_convert_fusion.s_ref
  48.6 7.0 %all-to-all-done.1 = bf16[16,22,2,3,128]{4,2,1,3,0:T(2,128)(2,1)S(1)} async-done(((bf16[16,22,2,3,128]{4,2,1,3,0:T(2,128)(2,1)}), bf16[16,22,2,3,128]{4,2,1,3,0:T(2,128)(2,1)S(1)}, u32[]{:S(2)}, u32[]{:S(2)}) %all-to-all-start.1) | async-done | bytes 540704 | tf_op jit(solution)/shard_map/all_to_all | solution.py:35
  55.7 0.4 copy.11
  56.0 0.4 fusion.5
  56.5 0.9 %copy.13 = bf16[3,22,32,128]{3,2,1,0:T(8,128)(2,1)} copy(bf16[3,22,32,128]{3,2,0,1:T(8,128)(2,1)S(1)} %fusion.5) | data formatting | bytes 1081344 | tf_op jit(solution)/shard_map/transpose | solution.py:103
  57.3 0.8 copy.12
  58.2 7.5 %shard_map.69 = bf16[2,704,1024]{2,1,0:T(8,128)(2,1)} custom-call(s32[1]{0:T(128)} %copy.14.lag_ref, bf16[3,704,128]{2,1,0:T(8,128)(2,1)} %bitcast.58, bf16[3,704,128]{2,1,0:T(8,128)(2,1)} %bitcast.56, bf16[128,1024]{1,0:T(8,128)(2,1)} %subtract_convert_fusion.s_ref), custom_call_target="tpu_custom_call" | custom-call | flops 1107296256 | bytes 4227072 | tf_op jit(solution)/shard_map/pallas_call | solution.py:67
  65.7 0.0 copy-start.1
  65.7 7.7 %shard_map.68 = bf16[2,704,1024]{2,1,0:T(8,128)(2,1)} custom-call(s32[1]{0:T(128)} %copy.14.lag_ref, bf16[3,704,128]{2,1,0:T(8,128)(2,1)} %bitcast.59, bf16[3,704,128]{2,1,0:T(8,128)(2,1)} %bitcast.57, bf16[128,1024]{1,0:T(8,128)(2,1)} %subtract_convert_fusion.1.s_ref), custom_call_target="tpu_custom_call" | custom-call | flops 1107296256 | bytes 4227072 | tf_op jit(solution)/shard_map/pallas_call | solution.py:67
  73.4 0.0 copy-done.1
  73.4 0.0 copy-start.2
  73.4 6.6 %fusion.3 = bf16[1,1024,1024]{2,1,0:T(8,128)(2,1)} fusion(f32[]{:T(128)S(6)} %convert_element_type.39, bf16[2,704,1024]{2,1,0:T(8,128)(2,1)} %shard_map.68, bf16[2,704,1024]{2,1,0:T(8,128)(2,1)S(1)} %copy-done.1), kind=kOutput, calls=%fused_computation.7 | convolution fusion | flops 2954887168 | bytes 7864324 | tf_op jit(solution)/shard_map/na,nb->ab/dot_general | solution.py:115
  80.0 0.0 copy-done.2
  80.0 4.7 %fusion.2 = bf16[1,1024,1024]{2,1,0:T(8,128)(2,1)} fusion(f32[]{:T(128)S(6)} %convert_element_type.39, bf16[2,704,1024]{2,1,0:T(8,128)(2,1)S(1)} %copy-done.2, bf16[2,704,1024]{2,1,0:T(8,128)(2,1)S(1)} %copy-done.1), kind=kOutput, calls=%fused_computation.6 | convolution fusion | flops 2954887168 | bytes 7864324 | tf_op jit(solution)/shard_map/na,nb->ab/dot_general | solution.py:111
  (5 shorter events, 0.1 us)
Async XLA Ops:
  0.6 0.9 %copy-start = (bf16[4,32,3,128]{3,1,2,0:T(8,128)(2,1)S(1)}, bf16[4,32,3,128]{3,1,2,0:T(8,128)(2,1)}, u32[]{:S(2)}) copy-start(bf16[4,32,3,128]{3,1,2,0:T(8,128)(2,1)} %param.5) | copy-start | bytes 294916
  2.3 35.4 %all-to-all-start = ((bf16[32,4,2,3,128]{4,2,3,1,0:T(2,128)(2,1)}), bf16[32,4,2,3,128]{4,2,3,1,0:T(2,128)(2,1)S(1)}, u32[]{:S(2)}, u32[]{:S(2)}) async-start(bf16[32,4,2,3,128]{4,2,3,1,0:T(2,128)(2,1)} %broadcast_in_dim.17), calls=%async_computation | async-start | bytes 393216 | tf_op jit(solution)/shard_map/all_to_all | solution.py:28
  39.6 16.1 %all-to-all-start.1 = ((bf16[16,22,2,3,128]{4,2,1,3,0:T(2,128)(2,1)}), bf16[16,22,2,3,128]{4,2,1,3,0:T(2,128)(2,1)S(1)}, u32[]{:S(2)}, u32[]{:S(2)}) async-start(bf16[16,22,2,3,128]{4,2,1,3,0:T(2,128)(2,1)} %broadcast_in_dim.19), calls=%async_computation.1 | async-start | bytes 1081344 | tf_op jit(solution)/shard_map/all_to_all | solution.py:35
  65.7 7.7 %copy-start.1 = (bf16[2,704,1024]{2,1,0:T(8,128)(2,1)S(1)}, bf16[2,704,1024]{2,1,0:T(8,128)(2,1)}, u32[]{:S(2)}) copy-start(bf16[2,704,1024]{2,1,0:T(8,128)(2,1)} %shard_map.69) | copy-start | bytes 8650756
  73.4 6.6 %copy-start.2 = (bf16[2,704,1024]{2,1,0:T(8,128)(2,1)S(1)}, bf16[2,704,1024]{2,1,0:T(8,128)(2,1)}, u32[]{:S(2)}) copy-start(bf16[2,704,1024]{2,1,0:T(8,128)(2,1)} %shard_map.68) | copy-start | bytes 8650756

commit v3 on v2

--- a/solution.py
+++ b/solution.py
@@ -11,7 +11,7 @@
 ATOMS = 128
 BLOCK_LEN = 32
 DRAWS = 22
-TILE = 256
+TILE = 512
 
 
 def gather_blocks(coordinates, resample, block_slot):
@@ -36,19 +36,16 @@
     return jnp.swapaxes(parts, 0, 1).reshape(DRAWS, BLOCK_LEN, 3, ATOMS)
 
 
-def centered_kernel(lag_ref, x_ref, xs_ref, s_ref, out_ref):
+def centered_kernel(planes, lag_ref, x_ref, s_ref, out_ref):
     lag = lag_ref[0]
     signed = s_ref[...]
-
-    def distances(ref):
-        total = None
-        for c in range(3):
-            d = jnp.dot(ref[c], signed, preferred_element_type=jnp.float32)
-            total = d * d if total is None else total + d * d
-        return jnp.sqrt(total).astype(jnp.bfloat16).astype(jnp.float32)
-
-    earlier = distances(x_ref)
-    later = distances(xs_ref)
+    total = None
+    for c in range(3):
+        d = jnp.dot(x_ref[c], signed, preferred_element_type=jnp.float32)
+        total = d * d if total is None else total + d * d
+    earlier = jnp.sqrt(total).astype(jnp.bfloat16).astype(jnp.float32)
+    n = earlier.shape[0]
+    later = pltpu.roll(earlier, n - lag, 0)
     rows = lax.broadcasted_iota(jnp.int32, earlier.shape, 0)
     valid = (rows % BLOCK_LEN) < (BLOCK_LEN - lag)
     earlier = jnp.where(valid, earlier, 0.0)
@@ -57,30 +54,32 @@
     mean = (
         jnp.sum(earlier, axis=0, keepdims=True) + jnp.sum(later, axis=0, keepdims=True)
     ) / count
-    out_ref[0] = jnp.where(valid, earlier - mean, 0.0).astype(jnp.bfloat16)
+    zero_lag = jnp.where(valid, earlier - mean, 0.0).astype(jnp.bfloat16)
+    out_ref[0] = zero_lag
     out_ref[1] = jnp.where(valid, later - mean, 0.0).astype(jnp.bfloat16)
+    if planes == 3:
+        out_ref[2] = zero_lag
 
 
-def centered_pairs(lag, frames, shifted, signed):
+def centered_pairs(lag, frames, signed, planes):
     n = frames.shape[1]
     width = signed.shape[1]
     return pl.pallas_call(
-        centered_kernel,
+        functools.partial(centered_kernel, planes),
         grid=(width // TILE,),
         in_specs=[
             pl.BlockSpec(memory_space=pltpu.SMEM),
             pl.BlockSpec((3, n, ATOMS), lambda j: (0, 0, 0)),
-            pl.BlockSpec((3, n, ATOMS), lambda j: (0, 0, 0)),
             pl.BlockSpec((ATOMS, TILE), lambda j: (0, j)),
         ],
-        out_specs=pl.BlockSpec((2, n, TILE), lambda j: (0, 0, j)),
-        out_shape=jax.ShapeDtypeStruct((2, n, width), jnp.bfloat16),
+        out_specs=pl.BlockSpec((planes, n, TILE), lambda j: (0, 0, j)),
+        out_shape=jax.ShapeDtypeStruct((planes, n, width), jnp.bfloat16),
         cost_estimate=pl.CostEstimate(
-            flops=2 * 2 * 3 * n * ATOMS * width,
-            transcendentals=2 * n * width,
-            bytes_accessed=2 * n * width * 2 + 2 * 3 * n * ATOMS * 2 + ATOMS * width * 2,
+            flops=2 * 3 * n * ATOMS * width,
+            transcendentals=n * width,
+            bytes_accessed=planes * n * width * 2 + 3 * n * ATOMS * 2 + ATOMS * width * 2,
         ),
-    )(lag, frames, shifted, signed)
+    )(lag, frames, signed)
 
 
 def signed_pairs(atom_pairs, first_feature, width):
@@ -97,22 +96,18 @@
     chosen = gather_blocks(coordinates, resample, block_slot)
     width = F // lax.axis_size("row")
     shift = lag_time[0]
-    doubled = jnp.concatenate([chosen, chosen], axis=1)
-    moved = lax.dynamic_slice_in_dim(doubled, shift, BLOCK_LEN, axis=1)
     frames = jnp.transpose(chosen, (2, 0, 1, 3)).reshape(3, DRAWS * BLOCK_LEN, ATOMS)
-    shifted = jnp.transpose(moved, (2, 0, 1, 3)).reshape(3, DRAWS * BLOCK_LEN, ATOMS)
     row_signed = signed_pairs(atom_pairs, lax.axis_index("row") * width, width)
     col_signed = signed_pairs(atom_pairs, lax.axis_index("col") * width, width)
-    row_stack = centered_pairs(lag_time, frames, shifted, row_signed)
-    col_stack = centered_pairs(lag_time, frames, shifted, col_signed)
+    row_stack = centered_pairs(lag_time, frames, row_signed, 2).reshape(-1, width)
+    col_stack = centered_pairs(lag_time, frames, col_signed, 3)
     pair_count = (2 * DRAWS * (BLOCK_LEN - shift)).astype(jnp.float32)
-    rows = row_stack.reshape(-1, width)
     instant = (
-        jnp.einsum("na,nb->ab", rows, col_stack.reshape(-1, width), preferred_element_type=jnp.float32)
+        jnp.einsum("na,nb->ab", row_stack, col_stack[:2].reshape(-1, width), preferred_element_type=jnp.float32)
         / pair_count
     )
     crossed = (
-        jnp.einsum("na,nb->ab", rows, col_stack[::-1].reshape(-1, width), preferred_element_type=jnp.float32)
+        jnp.einsum("na,nb->ab", row_stack, col_stack[1:].reshape(-1, width), preferred_element_type=jnp.float32)
         / pair_count
     )
     return (instant[None].astype(jnp.bfloat16), crossed[None].astype(jnp.bfloat16))

time: 85.9 us -> 85.3 us (level)
  no operation moved by 1% of the time
where the time goes in v3:
time: 85.3 us; the launch traced here: 84 us
  starting transfers between devices  23.5 us (28%)
  waiting for transfers between devices  21.4 us (25%)
  Pallas kernels  15.8 us (19%)
  matrix products  11.3 us (13%)
  local copies, waits for them, and re-layouts  6.86 us (8%)
  other arithmetic  3.72 us (4%)
  between operations  1.36 us (2%)
    all_to_all x1, starting transfers between devices, gather_blocks(): every = lax.all_to_all(spread, 'rep', 0, 0, tiled=True)  16.7 us
    pallas_call x2, Pallas kernels, centered_pairs(): pl.pallas_call(functools.partial(centered_kernel, planes), grid=(width //...  15.8 us
    all_to_all x1, waiting for transfers between devices, gather_blocks(): every = lax.all_to_all(spread, 'rep', 0, 0, tiled=True)  14.4 us
    all_to_all x1, waiting for transfers between devices, gather_blocks(): parts = lax.all_to_all(spread, ('row', 'col'), 0, 0, tiled=True)  7.06 us
    all_to_all x1, starting transfers between devices, gather_blocks(): parts = lax.all_to_all(spread, ('row', 'col'), 0, 0, tiled=True)  6.75 us
    dot_general x1, matrix products, shards(): jnp.einsum('na,nb->ab', row_stack, col_stack[1:].reshape(-1, width), pref...  6.62 us
    dot_general x1, matrix products, shards(): jnp.einsum('na,nb->ab', row_stack, col_stack[:2].reshape(-1, width), pref...  4.68 us
  transfers between devices with their start and end apart: 2, of which 2 were waited for; matrix products, arithmetic and copies ran while one was open for 7% of the time, Pallas kernels for 0%

profile of v3, /device:TPU:1, one launch (start us, length us, event | category | flops | bytes accessed | tf_op | source)
XLA Modules:
  0.0 84.0 jit_solution(16122159680483330253)
XLA Ops:
  0.6 0.0 copy-start
  0.7 0.9 %copy-done = bf16[4,32,3,128]{3,1,2,0:T(8,128)(2,1)S(1)} copy-done((bf16[4,32,3,128]{3,1,2,0:T(8,128)(2,1)S(1)}, bf16[4,32,3,128]{3,1,2,0:T(8,128)(2,1)}, u32[]{:S(2)}) %copy-start) | copy-done | bytes 98328
  1.5 0.8 broadcast_in_dim.17
  2.3 16.7 %all-to-all-start = ((bf16[32,4,2,3,128]{4,2,3,1,0:T(2,128)(2,1)}), bf16[32,4,2,3,128]{4,2,3,1,0:T(2,128)(2,1)S(1)}, u32[]{:S(2)}, u32[]{:S(2)}) async-start(bf16[32,4,2,3,128]{4,2,3,1,0:T(2,128)(2,1)} %broadcast_in_dim.17), calls=%async_computation | async-start | bytes 393216 | tf_op jit(solution)/shard_map/all_to_all | solution.py:28
  19.1 0.7 fusion.17
  19.8 1.4 %gather_fusion = s32[22]{0:T(128)S(1)} fusion(s32[128]{0:T(128)} %param.7, s32[1024]{0:T(1024)S(1)} %pad_clamp_fusion.1), kind=kCustom, calls=%fused_computation | custom fusion | bytes 264 | tf_op jit(solution)/shard_map/jit(_take)/gather | solution.py:30
  21.1 0.7 compare_and_fusion
  21.8 0.7 fusion.16
  22.5 0.9 %fusion.18 = (s32[1,4096]{1,0:T(1,128)S(1)}, s32[1,4096]{1,0:T(1,128)S(1)}) fusion(s32[2,4096]{1,0:T(2,128)} %param.9), kind=kLoop, calls=%fused_computation.35 | loop fusion | bytes 65536 | tf_op jit(solution)/shard_map/slice | solution.py:86
  23.3 14.4 %all-to-all-done = bf16[32,4,2,3,128]{4,2,3,1,0:T(2,128)(2,1)S(1)} async-done(((bf16[32,4,2,3,128]{4,2,3,1,0:T(2,128)(2,1)}), bf16[32,4,2,3,128]{4,2,3,1,0:T(2,128)(2,1)S(1)}, u32[]{:S(2)}, u32[]{:S(2)}) %all-to-all-start) | async-done | bytes 196640 | tf_op jit(solution)/shard_map/all_to_all | solution.py:28
  37.7 0.6 gather_fusion.1
  38.3 0.1 broadcast_select_fusion
  38.5 1.1 %broadcast_in_dim.19 = bf16[16,22,2,3,128]{4,2,1,3,0:T(2,128)(2,1)} broadcast(bf16[22,2,3,128]{3,1,0,2:T(2,128)(2,1)S(1)} %copy.10), dimensions={1,2,3,4} | broadcast | bytes 574464 | tf_op jit(solution)/shard_map/broadcast_in_dim | solution.py:34
  39.6 6.8 %all-to-all-start.1 = ((bf16[16,22,2,3,128]{4,2,1,3,0:T(2,128)(2,1)}), bf16[16,22,2,3,128]{4,2,1,3,0:T(2,128)(2,1)S(1)}, u32[]{:S(2)}, u32[]{:S(2)}) async-start(bf16[16,22,2,3,128]{4,2,1,3,0:T(2,128)(2,1)} %broadcast_in_dim.19), calls=%async_computation.1 | async-start | bytes 1081344 | tf_op jit(solution)/shard_map/all_to_all | solution.py:35
  47.0 0.8 subtract_convert_fusion.1.s_ref
  47.8 0.8 subtract_convert_fusion.s_ref
  48.6 7.1 %all-to-all-done.1 = bf16[16,22,2,3,128]{4,2,1,3,0:T(2,128)(2,1)S(1)} async-done(((bf16[16,22,2,3,128]{4,2,1,3,0:T(2,128)(2,1)}), bf16[16,22,2,3,128]{4,2,1,3,0:T(2,128)(2,1)S(1)}, u32[]{:S(2)}, u32[]{:S(2)}) %all-to-all-start.1) | async-done | bytes 540704 | tf_op jit(solution)/shard_map/all_to_all | solution.py:35
  55.7 0.4 copy.11
  56.0 0.8 %copy.12 = bf16[3,22,32,128]{3,2,1,0:T(8,128)(2,1)} copy(bf16[3,22,32,128]{3,2,0,1:T(8,128)(2,1)S(1)} %bitcast.50) | data formatting | bytes 1081344 | tf_op jit(solution)/shard_map/transpose | solution.py:99
  56.9 7.7 %shard_map.68 = bf16[2,704,1024]{2,1,0:T(8,128)(2,1)} custom-call(s32[1]{0:T(128)S(6)} %copy.13.lag_ref, bf16[3,704,128]{2,1,0:T(8,128)(2,1)} %bitcast.47, bf16[128,1024]{1,0:T(8,128)(2,1)} %subtract_convert_fusion.1.s_ref), custom_call_target="tpu_custom_call" | custom-call | flops 553648128 | bytes 3686400 | tf_op jit(solution)/shard_map/pallas_call | solution.py:67
  64.6 0.0 copy-start.2
  64.6 8.1 %shard_map.69 = bf16[3,704,1024]{2,1,0:T(8,128)(2,1)} custom-call(s32[1]{0:T(128)S(6)} %copy.13.lag_ref, bf16[3,704,128]{2,1,0:T(8,128)(2,1)} %bitcast.48, bf16[128,1024]{1,0:T(8,128)(2,1)} %subtract_convert_fusion.s_ref), custom_call_target="tpu_custom_call" | custom-call | flops 553648128 | bytes 5128192 | tf_op jit(solution)/shard_map/pallas_call | solution.py:67
  72.7 0.0 copy-done.2
  72.7 0.0 copy-start.1
  72.7 6.6 %fusion.13 = bf16[1,1024,1024]{2,1,0:T(8,128)(2,1)} fusion(f32[]{:T(128)} %bitcast.15, bf16[2,704,1024]{2,1,0:T(8,128)(2,1)S(1)} %copy-done.2, bf16[3,704,1024]{2,1,0:T(8,128)(2,1)} %shard_map.69), kind=kOutput, calls=%fused_computation.11 | convolution fusion | flops 2954887168 | bytes 7864832 | tf_op jit(solution)/shard_map/na,nb->ab/dot_general | solution.py:110
  79.4 0.0 copy-done.1
  79.4 4.7 %fusion.10 = bf16[1,1024,1024]{2,1,0:T(8,128)(2,1)} fusion(f32[]{:T(128)} %bitcast.15, bf16[2,704,1024]{2,1,0:T(8,128)(2,1)S(1)} %copy-done.2, bf16[3,704,1024]{2,1,0:T(8,128)(2,1)S(1)} %copy-done.1), kind=kOutput, calls=%fused_computation.10 | convolution fusion | flops 2954887168 | bytes 7864324 | tf_op jit(solution)/shard_map/na,nb->ab/dot_general | solution.py:106
  (5 shorter events, 0.1 us)
Async XLA Ops:
  0.6 0.9 %copy-start = (bf16[4,32,3,128]{3,1,2,0:T(8,128)(2,1)S(1)}, bf16[4,32,3,128]{3,1,2,0:T(8,128)(2,1)}, u32[]{:S(2)}) copy-start(bf16[4,32,3,128]{3,1,2,0:T(8,128)(2,1)} %param.5) | copy-start | bytes 294916
  2.3 35.4 %all-to-all-start = ((bf16[32,4,2,3,128]{4,2,3,1,0:T(2,128)(2,1)}), bf16[32,4,2,3,128]{4,2,3,1,0:T(2,128)(2,1)S(1)}, u32[]{:S(2)}, u32[]{:S(2)}) async-start(bf16[32,4,2,3,128]{4,2,3,1,0:T(2,128)(2,1)} %broadcast_in_dim.17), calls=%async_computation | async-start | bytes 393216 | tf_op jit(solution)/shard_map/all_to_all | solution.py:28
  39.6 16.1 %all-to-all-start.1 = ((bf16[16,22,2,3,128]{4,2,1,3,0:T(2,128)(2,1)}), bf16[16,22,2,3,128]{4,2,1,3,0:T(2,128)(2,1)S(1)}, u32[]{:S(2)}, u32[]{:S(2)}) async-start(bf16[16,22,2,3,128]{4,2,1,3,0:T(2,128)(2,1)} %broadcast_in_dim.19), calls=%async_computation.1 | async-start | bytes 1081344 | tf_op jit(solution)/shard_map/all_to_all | solution.py:35
  64.6 8.1 %copy-start.2 = (bf16[2,704,1024]{2,1,0:T(8,128)(2,1)S(1)}, bf16[2,704,1024]{2,1,0:T(8,128)(2,1)}, u32[]{:S(2)}) copy-start(bf16[2,704,1024]{2,1,0:T(8,128)(2,1)} %shard_map.68) | copy-start | bytes 8650756
  72.7 6.6 %copy-start.1 = (bf16[3,704,1024]{2,1,0:T(8,128)(2,1)S(1)}, bf16[3,704,1024]{2,1,0:T(8,128)(2,1)}, u32[]{:S(2)}) copy-start(bf16[3,704,1024]{2,1,0:T(8,128)(2,1)} %shard_map.69) | copy-start | bytes 12976132

commit v4 on v3

--- a/solution.py
+++ b/solution.py
@@ -36,29 +36,46 @@
     return jnp.swapaxes(parts, 0, 1).reshape(DRAWS, BLOCK_LEN, 3, ATOMS)
 
 
-def centered_kernel(planes, lag_ref, x_ref, s_ref, out_ref):
+def centered_kernel(planes, lag_ref, x_ref, s_ref, out_ref, diff_ref, dist_ref):
     lag = lag_ref[0]
     signed = s_ref[...]
-    total = None
     for c in range(3):
-        d = jnp.dot(x_ref[c], signed, preferred_element_type=jnp.float32)
-        total = d * d if total is None else total + d * d
-    earlier = jnp.sqrt(total).astype(jnp.bfloat16).astype(jnp.float32)
-    n = earlier.shape[0]
-    later = pltpu.roll(earlier, n - lag, 0)
-    rows = lax.broadcasted_iota(jnp.int32, earlier.shape, 0)
-    valid = (rows % BLOCK_LEN) < (BLOCK_LEN - lag)
-    earlier = jnp.where(valid, earlier, 0.0)
-    later = jnp.where(valid, later, 0.0)
+        diff_ref[c] = jnp.dot(x_ref[c], signed, preferred_element_type=jnp.float32)
+    width = signed.shape[1]
+    frame = lax.broadcasted_iota(jnp.int32, (BLOCK_LEN, width), 0)
+    first = frame < BLOCK_LEN - lag
+    second = frame >= lag
+    dist_ref[pl.ds(DRAWS * BLOCK_LEN, BLOCK_LEN), :] = jnp.zeros((BLOCK_LEN, width), jnp.float32)
+
+    def distances(d, sums):
+        rows = pl.ds(pl.multiple_of(d * BLOCK_LEN, BLOCK_LEN), BLOCK_LEN)
+        total = None
+        for c in range(3):
+            part = diff_ref[c, rows, :]
+            total = part * part if total is None else total + part * part
+        dist = jnp.sqrt(total).astype(jnp.bfloat16).astype(jnp.float32)
+        dist_ref[rows, :] = dist
+        picked = jnp.where(first, dist, 0.0) + jnp.where(second, dist, 0.0)
+        return sums + picked.reshape(BLOCK_LEN // 8, 8, width).sum(axis=0)
+
+    sums = lax.fori_loop(0, DRAWS, distances, jnp.zeros((8, width), jnp.float32))
     count = (2 * DRAWS * (BLOCK_LEN - lag)).astype(jnp.float32)
-    mean = (
-        jnp.sum(earlier, axis=0, keepdims=True) + jnp.sum(later, axis=0, keepdims=True)
-    ) / count
-    zero_lag = jnp.where(valid, earlier - mean, 0.0).astype(jnp.bfloat16)
-    out_ref[0] = zero_lag
-    out_ref[1] = jnp.where(valid, later - mean, 0.0).astype(jnp.bfloat16)
-    if planes == 3:
-        out_ref[2] = zero_lag
+    mean = jnp.sum(sums, axis=0, keepdims=True) / count
+
+    def center(d, carry):
+        start = pl.multiple_of(d * BLOCK_LEN, BLOCK_LEN)
+        rows = pl.ds(start, BLOCK_LEN)
+        earlier = dist_ref[rows, :]
+        window = dist_ref[pl.ds(start, 2 * BLOCK_LEN), :]
+        later = pltpu.roll(window, 2 * BLOCK_LEN - lag, 0)[:BLOCK_LEN]
+        zero_lag = jnp.where(first, earlier - mean, 0.0).astype(jnp.bfloat16)
+        out_ref[0, rows, :] = zero_lag
+        out_ref[1, rows, :] = jnp.where(first, later - mean, 0.0).astype(jnp.bfloat16)
+        if planes == 3:
+            out_ref[2, rows, :] = zero_lag
+        return carry
+
+    lax.fori_loop(0, DRAWS, center, 0)
 
 
 def centered_pairs(lag, frames, signed, planes):
@@ -74,6 +91,10 @@
         ],
         out_specs=pl.BlockSpec((planes, n, TILE), lambda j: (0, 0, j)),
         out_shape=jax.ShapeDtypeStruct((planes, n, width), jnp.bfloat16),
+        scratch_shapes=[
+            pltpu.VMEM((3, n, TILE), jnp.float32),
+            pltpu.VMEM((n + BLOCK_LEN, TILE), jnp.float32),
+        ],
         cost_estimate=pl.CostEstimate(
             flops=2 * 3 * n * ATOMS * width,
             transcendentals=n * width,

time: 85.3 us -> 84.7 us (level)
  no operation moved by 1% of the time
where the time goes in v4:
time: 84.7 us; the launch traced here: 83.4 us
  starting transfers between devices  23.5 us (28%)
  waiting for transfers between devices  21.4 us (25%)
  Pallas kernels  15.2 us (18%)
  matrix products  11.3 us (13%)
  local copies, waits for them, and re-layouts  6.86 us (8%)
  other arithmetic  3.72 us (4%)
  between operations  1.36 us (2%)
    all_to_all x1, starting transfers between devices, gather_blocks(): every = lax.all_to_all(spread, 'rep', 0, 0, tiled=True)  16.7 us
    pallas_call x2, Pallas kernels, centered_pairs(): pl.pallas_call(functools.partial(centered_kernel, planes), grid=(width //...  15.2 us
    all_to_all x1, waiting for transfers between devices, gather_blocks(): every = lax.all_to_all(spread, 'rep', 0, 0, tiled=True)  14.4 us
    all_to_all x1, waiting for transfers between devices, gather_blocks(): parts = lax.all_to_all(spread, ('row', 'col'), 0, 0, tiled=True)  7.06 us
    all_to_all x1, starting transfers between devices, gather_blocks(): parts = lax.all_to_all(spread, ('row', 'col'), 0, 0, tiled=True)  6.75 us
    dot_general x1, matrix products, shards(): jnp.einsum('na,nb->ab', row_stack, col_stack[1:].reshape(-1, width), pref...  6.62 us
    dot_general x1, matrix products, shards(): jnp.einsum('na,nb->ab', row_stack, col_stack[:2].reshape(-1, width), pref...  4.69 us
  transfers between devices with their start and end apart: 2, of which 2 were waited for; matrix products, arithmetic and copies ran while one was open for 7% of the time, Pallas kernels for 0%

profile of v4, /device:TPU:1, one launch (start us, length us, event | category | flops | bytes accessed | tf_op | source)
XLA Modules:
  0.0 83.4 jit_solution(13250814316301510247)
XLA Ops:
  0.6 0.0 copy-start
  0.7 0.9 %copy-done = bf16[4,32,3,128]{3,1,2,0:T(8,128)(2,1)S(1)} copy-done((bf16[4,32,3,128]{3,1,2,0:T(8,128)(2,1)S(1)}, bf16[4,32,3,128]{3,1,2,0:T(8,128)(2,1)}, u32[]{:S(2)}) %copy-start) | copy-done | bytes 98328
  1.5 0.8 broadcast_in_dim.17
  2.3 16.7 %all-to-all-start = ((bf16[32,4,2,3,128]{4,2,3,1,0:T(2,128)(2,1)}), bf16[32,4,2,3,128]{4,2,3,1,0:T(2,128)(2,1)S(1)}, u32[]{:S(2)}, u32[]{:S(2)}) async-start(bf16[32,4,2,3,128]{4,2,3,1,0:T(2,128)(2,1)} %broadcast_in_dim.17), calls=%async_computation | async-start | bytes 393216 | tf_op jit(solution)/shard_map/all_to_all | solution.py:28
  19.1 0.7 fusion.17
  19.8 1.4 %gather_fusion = s32[22]{0:T(128)S(1)} fusion(s32[128]{0:T(128)} %param.7, s32[1024]{0:T(1024)S(1)} %pad_clamp_fusion.1), kind=kCustom, calls=%fused_computation | custom fusion | bytes 264 | tf_op jit(solution)/shard_map/jit(_take)/gather | solution.py:30
  21.1 0.7 compare_and_fusion
  21.8 0.7 fusion.16
  22.5 0.9 %fusion.18 = (s32[1,4096]{1,0:T(1,128)S(1)}, s32[1,4096]{1,0:T(1,128)S(1)}) fusion(s32[2,4096]{1,0:T(2,128)} %param.9), kind=kLoop, calls=%fused_computation.35 | loop fusion | bytes 65536 | tf_op jit(solution)/shard_map/slice | solution.py:107
  23.3 14.4 %all-to-all-done = bf16[32,4,2,3,128]{4,2,3,1,0:T(2,128)(2,1)S(1)} async-done(((bf16[32,4,2,3,128]{4,2,3,1,0:T(2,128)(2,1)}), bf16[32,4,2,3,128]{4,2,3,1,0:T(2,128)(2,1)S(1)}, u32[]{:S(2)}, u32[]{:S(2)}) %all-to-all-start) | async-done | bytes 196640 | tf_op jit(solution)/shard_map/all_to_all | solution.py:28
  37.7 0.6 gather_fusion.1
  38.3 0.1 broadcast_select_fusion
  38.5 1.1 %broadcast_in_dim.19 = bf16[16,22,2,3,128]{4,2,1,3,0:T(2,128)(2,1)} broadcast(bf16[22,2,3,128]{3,1,0,2:T(2,128)(2,1)S(1)} %copy.10), dimensions={1,2,3,4} | broadcast | bytes 574464 | tf_op jit(solution)/shard_map/broadcast_in_dim | solution.py:34
  39.6 6.8 %all-to-all-start.1 = ((bf16[16,22,2,3,128]{4,2,1,3,0:T(2,128)(2,1)}), bf16[16,22,2,3,128]{4,2,1,3,0:T(2,128)(2,1)S(1)}, u32[]{:S(2)}, u32[]{:S(2)}) async-start(bf16[16,22,2,3,128]{4,2,1,3,0:T(2,128)(2,1)} %broadcast_in_dim.19), calls=%async_computation.1 | async-start | bytes 1081344 | tf_op jit(solution)/shard_map/all_to_all | solution.py:35
  47.0 0.8 subtract_convert_fusion.1.s_ref
  47.8 0.8 subtract_convert_fusion.s_ref
  48.6 7.1 %all-to-all-done.1 = bf16[16,22,2,3,128]{4,2,1,3,0:T(2,128)(2,1)S(1)} async-done(((bf16[16,22,2,3,128]{4,2,1,3,0:T(2,128)(2,1)}), bf16[16,22,2,3,128]{4,2,1,3,0:T(2,128)(2,1)S(1)}, u32[]{:S(2)}, u32[]{:S(2)}) %all-to-all-start.1) | async-done | bytes 540704 | tf_op jit(solution)/shard_map/all_to_all | solution.py:35
  55.7 0.4 copy.11
  56.0 0.8 %copy.12 = bf16[3,22,32,128]{3,2,1,0:T(8,128)(2,1)} copy(bf16[3,22,32,128]{3,2,0,1:T(8,128)(2,1)S(1)} %bitcast.50) | data formatting | bytes 1081344 | tf_op jit(solution)/shard_map/transpose | solution.py:120
  56.9 7.4 %shard_map.68 = bf16[2,704,1024]{2,1,0:T(8,128)(2,1)} custom-call(s32[1]{0:T(128)S(6)} %copy.13.lag_ref, bf16[3,704,128]{2,1,0:T(8,128)(2,1)} %bitcast.47, bf16[128,1024]{1,0:T(8,128)(2,1)} %subtract_convert_fusion.1.s_ref), custom_call_target="tpu_custom_call" | custom-call | flops 553648128 | bytes 3686400 | tf_op jit(solution)/shard_map/pallas_call | solution.py:84
  64.3 0.0 copy-start.2
  64.3 7.8 %shard_map.69 = bf16[3,704,1024]{2,1,0:T(8,128)(2,1)} custom-call(s32[1]{0:T(128)S(6)} %copy.13.lag_ref, bf16[3,704,128]{2,1,0:T(8,128)(2,1)} %bitcast.48, bf16[128,1024]{1,0:T(8,128)(2,1)} %subtract_convert_fusion.s_ref), custom_call_target="tpu_custom_call" | custom-call | flops 553648128 | bytes 5128192 | tf_op jit(solution)/shard_map/pallas_call | solution.py:84
  72.1 0.0 copy-done.2
  72.1 0.0 copy-start.1
  72.1 6.6 %fusion.13 = bf16[1,1024,1024]{2,1,0:T(8,128)(2,1)} fusion(f32[]{:T(128)} %bitcast.15, bf16[2,704,1024]{2,1,0:T(8,128)(2,1)S(1)} %copy-done.2, bf16[3,704,1024]{2,1,0:T(8,128)(2,1)} %shard_map.69), kind=kOutput, calls=%fused_computation.11 | convolution fusion | flops 2954887168 | bytes 7864832 | tf_op jit(solution)/shard_map/na,nb->ab/dot_general | solution.py:131
  78.8 0.0 copy-done.1
  78.8 4.7 %fusion.10 = bf16[1,1024,1024]{2,1,0:T(8,128)(2,1)} fusion(f32[]{:T(128)} %bitcast.15, bf16[2,704,1024]{2,1,0:T(8,128)(2,1)S(1)} %copy-done.2, bf16[3,704,1024]{2,1,0:T(8,128)(2,1)S(1)} %copy-done.1), kind=kOutput, calls=%fused_computation.10 | convolution fusion | flops 2954887168 | bytes 7864324 | tf_op jit(solution)/shard_map/na,nb->ab/dot_general | solution.py:127
  (5 shorter events, 0.1 us)
Async XLA Ops:
  0.6 0.9 %copy-start = (bf16[4,32,3,128]{3,1,2,0:T(8,128)(2,1)S(1)}, bf16[4,32,3,128]{3,1,2,0:T(8,128)(2,1)}, u32[]{:S(2)}) copy-start(bf16[4,32,3,128]{3,1,2,0:T(8,128)(2,1)} %param.5) | copy-start | bytes 294916
  2.3 35.4 %all-to-all-start = ((bf16[32,4,2,3,128]{4,2,3,1,0:T(2,128)(2,1)}), bf16[32,4,2,3,128]{4,2,3,1,0:T(2,128)(2,1)S(1)}, u32[]{:S(2)}, u32[]{:S(2)}) async-start(bf16[32,4,2,3,128]{4,2,3,1,0:T(2,128)(2,1)} %broadcast_in_dim.17), calls=%async_computation | async-start | bytes 393216 | tf_op jit(solution)/shard_map/all_to_all | solution.py:28
  39.6 16.1 %all-to-all-start.1 = ((bf16[16,22,2,3,128]{4,2,1,3,0:T(2,128)(2,1)}), bf16[16,22,2,3,128]{4,2,1,3,0:T(2,128)(2,1)S(1)}, u32[]{:S(2)}, u32[]{:S(2)}) async-start(bf16[16,22,2,3,128]{4,2,1,3,0:T(2,128)(2,1)} %broadcast_in_dim.19), calls=%async_computation.1 | async-start | bytes 1081344 | tf_op jit(solution)/shard_map/all_to_all | solution.py:35
  64.3 7.8 %copy-start.2 = (bf16[2,704,1024]{2,1,0:T(8,128)(2,1)S(1)}, bf16[2,704,1024]{2,1,0:T(8,128)(2,1)}, u32[]{:S(2)}) copy-start(bf16[2,704,1024]{2,1,0:T(8,128)(2,1)} %shard_map.68) | copy-start | bytes 8650756
  72.1 6.6 %copy-start.1 = (bf16[3,704,1024]{2,1,0:T(8,128)(2,1)S(1)}, bf16[3,704,1024]{2,1,0:T(8,128)(2,1)}, u32[]{:S(2)}) copy-start(bf16[3,704,1024]{2,1,0:T(8,128)(2,1)} %shard_map.69) | copy-start | bytes 12976132

commit v5 on v3

v5 whole, which is shorter than its diff:
```python
import functools

import jax
import jax.numpy as jnp
from jax import lax
from jax.experimental import pallas as pl
from jax.experimental.pallas import tpu as pltpu
from jax.sharding import PartitionSpec as P

F = 4096
ATOMS = 128
BLOCK_LEN = 32
DRAWS = 22
CHUNK = 128
OUT_BLOCK = 256


def gather_blocks(coordinates, resample, block_slot):
    groups = lax.axis_size("row") * lax.axis_size("col")
    if BLOCK_LEN % groups:
        groups = 1
    frames = BLOCK_LEN // groups
    member = lax.axis_index("row") * lax.axis_size("col") + lax.axis_index("col")
    if groups == 1:
        member = 0
    piece = lax.dynamic_slice_in_dim(coordinates, member * frames, frames, axis=1)
    reps = lax.axis_size("rep")
    spread = jnp.broadcast_to(piece[None], (reps,) + piece.shape)
    every = lax.all_to_all(spread, "rep", 0, 0, tiled=True)
    every = every.reshape((-1,) + piece.shape[1:])
    slots = jnp.take(block_slot, resample[0], axis=0)
    picked = jnp.take(every, slots, axis=0)
    if groups == 1:
        return picked
    spread = jnp.broadcast_to(picked[None], (groups,) + picked.shape)
    parts = lax.all_to_all(spread, ("row", "col"), 0, 0, tiled=True)
    return jnp.swapaxes(parts, 0, 1).reshape(DRAWS, BLOCK_LEN, 3, ATOMS)


def covariance_kernel(lag_ref, x_ref, sr_ref, sc_ref, inst_ref, cross_ref, stack_ref):
    lag = lag_ref[0]
    lanes = x_ref.shape[2]
    count = (2 * DRAWS * (BLOCK_LEN - lag)).astype(jnp.float32)

    @pl.when(pl.program_id(0) == 0)
    def _():
        pair = lax.broadcasted_iota(jnp.int32, (1, lanes), 1)
        first = ((pair % BLOCK_LEN) < (BLOCK_LEN - lag)) & (pair < DRAWS * BLOCK_LEN)

        per_tile = sr_ref.shape[0] // CHUNK

        def centered(i, carry):
            tile = i // per_tile
            start = pl.multiple_of((i % per_tile) * CHUNK, CHUNK)
            rows = pl.ds(start, CHUNK)
            signed = jnp.where(tile == 0, sr_ref[rows, :], sc_ref[rows, :])
            total = None
            for c in range(3):
                d = jnp.dot(signed, x_ref[c], preferred_element_type=jnp.float32)
                total = d * d if total is None else total + d * d
            dist = jnp.sqrt(total).astype(jnp.bfloat16).astype(jnp.float32)
            later = pltpu.roll(dist, lanes - lag, 1)
            earlier = jnp.where(first, dist, 0.0)
            later = jnp.where(first, later, 0.0)
            mean = (
                jnp.sum(earlier, axis=1, keepdims=True) + jnp.sum(later, axis=1, keepdims=True)
            ) / count
            stack_ref[2 * tile, rows, :] = jnp.where(first, earlier - mean, 0.0).astype(jnp.bfloat16)
            stack_ref[2 * tile + 1, rows, :] = jnp.where(first, later - mean, 0.0).astype(jnp.bfloat16)
            return carry

        lax.fori_loop(0, 2 * per_tile, centered, 0)

    block = inst_ref.shape[0]
    rows = pl.ds(pl.multiple_of(pl.program_id(0) * block, block), block)
    nt = (((1,), (1,)), ((), ()))
    zero_row = stack_ref[0, rows, :]
    lag_row = stack_ref[1, rows, :]
    zero_col = stack_ref[2]
    lag_col = stack_ref[3]
    instant = lax.dot_general(zero_row, zero_col, nt, preferred_element_type=jnp.float32)
    instant = instant + lax.dot_general(lag_row, lag_col, nt, preferred_element_type=jnp.float32)
    inst_ref[...] = (instant / count).astype(inst_ref.dtype)
    crossed = lax.dot_general(zero_row, lag_col, nt, preferred_element_type=jnp.float32)
    crossed = crossed + lax.dot_general(lag_row, zero_col, nt, preferred_element_type=jnp.float32)
    cross_ref[...] = (crossed / count).astype(cross_ref.dtype)


def covariances(lag, frames, row_signed, col_signed):
    lanes = frames.shape[2]
    width = row_signed.shape[0]
    out = jax.ShapeDtypeStruct((width, width), jnp.bfloat16)
    return pl.pallas_call(
        covariance_kernel,
        grid=(width // OUT_BLOCK,),
        in_specs=[
            pl.BlockSpec(memory_space=pltpu.SMEM),
            pl.BlockSpec((3, ATOMS, lanes), lambda j: (0, 0, 0)),
            pl.BlockSpec((width, ATOMS), lambda j: (0, 0)),
            pl.BlockSpec((width, ATOMS), lambda j: (0, 0)),
        ],
        out_specs=[
            pl.BlockSpec((OUT_BLOCK, width), lambda j: (j, 0)),
            pl.BlockSpec((OUT_BLOCK, width), lambda j: (j, 0)),
        ],
        out_shape=[out, out],
        scratch_shapes=[pltpu.VMEM((4, width, lanes), jnp.bfloat16)],
        compiler_params=pltpu.CompilerParams(dimension_semantics=("arbitrary",)),
        cost_estimate=pl.CostEstimate(
            flops=2 * 2 * 3 * width * ATOMS * lanes + 4 * 2 * width * width * lanes,
            transcendentals=2 * width * lanes,
            bytes_accessed=2 * width * width * 2 + 3 * ATOMS * lanes * 2 + 2 * width * ATOMS * 2,
        ),
    )(lag, frames, row_signed, col_signed)


def signed_pairs(atom_pairs, first_feature, width):
    first_atoms = lax.dynamic_slice_in_dim(atom_pairs[0], first_feature, width)
    second_atoms = lax.dynamic_slice_in_dim(atom_pairs[1], first_feature, width)
    atom_ids = jnp.arange(ATOMS, dtype=jnp.int32)[None, :]
    return (
        (first_atoms[:, None] == atom_ids).astype(jnp.float32)
        - (second_atoms[:, None] == atom_ids).astype(jnp.float32)
    ).astype(jnp.bfloat16)


def shards(coordinates, resample, block_slot, lag_time, atom_pairs):
    chosen = gather_blocks(coordinates, resample, block_slot)
    width = F // lax.axis_size("row")
    pairs = DRAWS * BLOCK_LEN
    lanes = -(-pairs // 128) * 128
    frames = jnp.transpose(chosen, (2, 3, 0, 1)).reshape(3, ATOMS, pairs)
    frames = jnp.pad(frames, ((0, 0), (0, 0), (0, lanes - pairs)))
    row_signed = signed_pairs(atom_pairs, lax.axis_index("row") * width, width)
    col_signed = signed_pairs(atom_pairs, lax.axis_index("col") * width, width)
    instant, crossed = covariances(lag_time, frames, row_signed, col_signed)
    return (instant[None], crossed[None])


def solution(mesh):
    return jax.shard_map(
        shards,
        mesh=mesh,
        in_specs=(P("rep", None, None, None), P("rep", None), P(), P("rep"), P()),
        out_specs=(P("rep", "row", "col"), P("rep", "row", "col")),
        check_vma=False,
    )
```

time: 85.3 us -> 77.6 us (0.910)
  matrix products: 11.3 us -> 0 us
  Pallas kernels: 15.8 us -> 19.2 us
    dot_general x2 -> x0, matrix products: 11.3 us -> none  [the longest x1 6.62 us: shards(): jnp.einsum('na,nb->ab', row_stack, col_stack[1:].reshape(-1, width), pref...]
    pallas_call x2 -> x1, Pallas kernels: 15.8 us -> 19.2 us  [covariances(): pl.pallas_call(covariance_kernel, grid=(width // OUT_BLOCK,), in_specs=[p...]
    pad x0 -> x1, local copies, waits for them, and re-layouts: none -> 0.87 us  [shards(): frames = jnp.pad(frames, ((0, 0), (0, 0), (0, lanes - pairs)))]
  transfers between devices with their start and end apart: 2 -> 2, of which waited for: 2 -> 2; matrix products, arithmetic and copies ran while one was open for 7% -> 8% of each run, Pallas kernels for 0% -> 0%
where the time goes in v5:
time: 77.6 us; the launch traced here: 76.4 us
  starting transfers between devices  23.5 us (30%)
  waiting for transfers between devices  21 us (27%)
  Pallas kernels  19.2 us (25%)
  local copies, waits for them, and re-layouts  7.13 us (9%)
  other arithmetic  4.2 us (5%)
  between operations  1.36 us (2%)
    pallas_call x1, Pallas kernels, covariances(): pl.pallas_call(covariance_kernel, grid=(width // OUT_BLOCK,), in_specs=[p...  19.2 us
    all_to_all x1, starting transfers between devices, gather_blocks(): every = lax.all_to_all(spread, 'rep', 0, 0, tiled=True)  16.7 us
    all_to_all x1, waiting for transfers between devices, gather_blocks(): every = lax.all_to_all(spread, 'rep', 0, 0, tiled=True)  14.4 us
    all_to_all x1, starting transfers between devices, gather_blocks(): parts = lax.all_to_all(spread, ('row', 'col'), 0, 0, tiled=True)  6.75 us
    all_to_all x1, waiting for transfers between devices, gather_blocks(): parts = lax.all_to_all(spread, ('row', 'col'), 0, 0, tiled=True)  6.59 us
    convert_element_type x2, other arithmetic, signed_pairs(): return ((first_atoms[:, None] == atom_ids).astype(jnp.float32) - (second_...  2.08 us
  transfers between devices with their start and end apart: 2, of which 2 were waited for; matrix products, arithmetic and copies ran while one was open for 8% of the time, Pallas kernels for 0%

profile of v5, /device:TPU:1, one launch (start us, length us, event | category | flops | bytes accessed | tf_op | source)
XLA Modules:
  0.0 76.4 jit_solution(758884388548465008)
XLA Ops:
  0.6 0.0 copy-start
  0.7 0.9 %copy-done = bf16[4,32,3,128]{3,1,2,0:T(8,128)(2,1)S(1)} copy-done((bf16[4,32,3,128]{3,1,2,0:T(8,128)(2,1)S(1)}, bf16[4,32,3,128]{3,1,2,0:T(8,128)(2,1)}, u32[]{:S(2)}) %copy-start) | copy-done | bytes 98328
  1.5 0.8 %broadcast_in_dim.21 = bf16[32,4,2,3,128]{4,2,3,1,0:T(2,128)(2,1)} broadcast(bf16[4,2,3,128]{3,1,2,0:T(2,128)(2,1)S(1)} %constant_dynamic-slice_fusion.4), dimensions={1,2,3,4} | broadcast | bytes 202752 | tf_op jit(solution)/shard_map/broadcast_in_dim | solution.py:28
  2.3 16.7 %all-to-all-start = ((bf16[32,4,2,3,128]{4,2,3,1,0:T(2,128)(2,1)}), bf16[32,4,2,3,128]{4,2,3,1,0:T(2,128)(2,1)S(1)}, u32[]{:S(2)}, u32[]{:S(2)}) async-start(bf16[32,4,2,3,128]{4,2,3,1,0:T(2,128)(2,1)} %broadcast_in_dim.21), calls=%async_computation | async-start | bytes 393216 | tf_op jit(solution)/shard_map/all_to_all | solution.py:29
  19.1 0.7 fusion.1
  19.8 1.4 %gather_fusion = s32[22]{0:T(128)S(1)} fusion(s32[128]{0:T(128)} %param.7, s32[1024]{0:T(1024)S(1)} %pad_clamp_fusion.1), kind=kCustom, calls=%fused_computation | custom fusion | bytes 264 | tf_op jit(solution)/shard_map/jit(_take)/gather | solution.py:31
  21.1 0.7 compare_and_fusion
  21.8 0.7 fusion
  22.5 0.9 %fusion.2 = (s32[1,4096]{1,0:T(1,128)S(1)}, s32[1,4096]{1,0:T(1,128)S(1)}) fusion(s32[2,4096]{1,0:T(2,128)} %param.9), kind=kLoop, calls=%fused_computation.25 | loop fusion | bytes 65536 | tf_op jit(solution)/shard_map/slice | solution.py:118
  23.3 14.4 %all-to-all-done = bf16[32,4,2,3,128]{4,2,3,1,0:T(2,128)(2,1)S(1)} async-done(((bf16[32,4,2,3,128]{4,2,3,1,0:T(2,128)(2,1)}), bf16[32,4,2,3,128]{4,2,3,1,0:T(2,128)(2,1)S(1)}, u32[]{:S(2)}, u32[]{:S(2)}) %all-to-all-start) | async-done | bytes 196640 | tf_op jit(solution)/shard_map/all_to_all | solution.py:29
  37.7 0.6 gather_fusion.1
  38.3 0.1 broadcast_select_fusion
  38.4 1.1 %broadcast_in_dim.23 = bf16[16,22,2,3,128]{4,2,3,1,0:T(2,128)(2,1)} broadcast(bf16[22,2,3,128]{3,1,2,0:T(2,128)(2,1)S(1)} %broadcast_select_fusion), dimensions={1,2,3,4} | broadcast | bytes 574464 | tf_op jit(solution)/shard_map/broadcast_in_dim | solution.py:35
  39.5 6.8 %all-to-all-start.1 = ((bf16[16,22,2,3,128]{4,2,3,1,0:T(2,128)(2,1)}), bf16[16,22,2,3,128]{4,2,3,1,0:T(2,128)(2,1)S(1)}, u32[]{:S(2)}, u32[]{:S(2)}) async-start(bf16[16,22,2,3,128]{4,2,3,1,0:T(2,128)(2,1)} %broadcast_in_dim.23), calls=%async_computation.1 | async-start | bytes 1081344 | tf_op jit(solution)/shard_map/all_to_all | solution.py:36
  47.0 1.0 %subtract_convert_fusion.1.sr_ref = bf16[1024,128]{1,0:T(8,128)(2,1)} fusion(s32[1024]{0:T(1024)S(1)} %bitcast.36, s32[1024]{0:T(1024)S(1)} %bitcast.37), kind=kLoop, calls=%fused_computation.5 | loop fusion | flops 786432 | bytes 270336 | tf_op jit(solution)/shard_map/convert_element_type | solution.py:124
  48.0 1.0 %subtract_convert_fusion.sc_ref = bf16[1024,128]{1,0:T(8,128)(2,1)} fusion(s32[1024]{0:T(1024)S(1)} %bitcast.34, s32[1024]{0:T(1024)S(1)} %bitcast.35), kind=kLoop, calls=%fused_computation.2 | loop fusion | flops 786432 | bytes 270336 | tf_op jit(solution)/shard_map/convert_element_type | solution.py:124
  49.0 6.6 %all-to-all-done.1 = bf16[16,22,2,3,128]{4,2,3,1,0:T(2,128)(2,1)S(1)} async-done(((bf16[16,22,2,3,128]{4,2,3,1,0:T(2,128)(2,1)}), bf16[16,22,2,3,128]{4,2,3,1,0:T(2,128)(2,1)S(1)}, u32[]{:S(2)}, u32[]{:S(2)}) %all-to-all-start.1) | async-done | bytes 540704 | tf_op jit(solution)/shard_map/all_to_all | solution.py:36
  55.6 0.4 copy.10
  56.1 0.2 copy.12
  56.3 0.9 %pad.4.x_ref = bf16[3,128,768]{2,1,0:T(8,128)(2,1)} pad(bf16[3,128,704]{2,1,0:T(8,128)(2,1)S(1)} %copy.12, bf16[]{:T(256)} %constant.50.clone.1), padding=0_0x0_0x0_64 | pad | bytes 1130498 | tf_op jit(solution)/shard_map/jit(_pad)/pad | solution.py:133
  57.2 19.2 %shard_map.68 = (bf16[1024,1024]{1,0:T(8,128)(2,1)}, bf16[1024,1024]{1,0:T(8,128)(2,1)}) custom-call(s32[1]{0:T(128)S(6)} %copy.13.lag_ref, bf16[3,128,768]{2,1,0:T(8,128)(2,1)} %pad.4.x_ref, bf16[1024,128]{1,0:T(8,128)(2,1)} %subtract_convert_fusion.1.sr_ref, bf16[1024,128]{1,0:T(8,128)(2,1)} %subtract_convert_fusion.sc_ref), custom_call_target="tpu_custom_call" | custom-call | flops 7650410496 | bytes 5308416 | tf_op jit(solution)/shard_map/pallas_call | solution.py:93
  (5 shorter events, 0.1 us)
Async XLA Ops:
  0.6 0.9 %copy-start = (bf16[4,32,3,128]{3,1,2,0:T(8,128)(2,1)S(1)}, bf16[4,32,3,128]{3,1,2,0:T(8,128)(2,1)}, u32[]{:S(2)}) copy-start(bf16[4,32,3,128]{3,1,2,0:T(8,128)(2,1)} %param.5) | copy-start | bytes 294916
  2.3 35.4 %all-to-all-start = ((bf16[32,4,2,3,128]{4,2,3,1,0:T(2,128)(2,1)}), bf16[32,4,2,3,128]{4,2,3,1,0:T(2,128)(2,1)S(1)}, u32[]{:S(2)}, u32[]{:S(2)}) async-start(bf16[32,4,2,3,128]{4,2,3,1,0:T(2,128)(2,1)} %broadcast_in_dim.21), calls=%async_computation | async-start | bytes 393216 | tf_op jit(solution)/shard_map/all_to_all | solution.py:29
  39.5 16.1 %all-to-all-start.1 = ((bf16[16,22,2,3,128]{4,2,3,1,0:T(2,128)(2,1)}), bf16[16,22,2,3,128]{4,2,3,1,0:T(2,128)(2,1)S(1)}, u32[]{:S(2)}, u32[]{:S(2)}) async-start(bf16[16,22,2,3,128]{4,2,3,1,0:T(2,128)(2,1)} %broadcast_in_dim.23), calls=%async_computation.1 | async-start | bytes 1081344 | tf_op jit(solution)/shard_map/all_to_all | solution.py:36

commit v6 on v5

--- a/solution.py
+++ b/solution.py
@@ -37,7 +37,7 @@
     return jnp.swapaxes(parts, 0, 1).reshape(DRAWS, BLOCK_LEN, 3, ATOMS)
 
 
-def covariance_kernel(lag_ref, x_ref, sr_ref, sc_ref, inst_ref, cross_ref, stack_ref):
+def covariance_kernel(lag_ref, x_ref, mask_ref, sr_ref, sc_ref, inst_ref, cross_ref, row_ref, col_ref, swap_ref):
     lag = lag_ref[0]
     lanes = x_ref.shape[2]
     count = (2 * DRAWS * (BLOCK_LEN - lag)).astype(jnp.float32)
@@ -46,47 +46,51 @@
     def _():
         pair = lax.broadcasted_iota(jnp.int32, (1, lanes), 1)
         first = ((pair % BLOCK_LEN) < (BLOCK_LEN - lag)) & (pair < DRAWS * BLOCK_LEN)
-
         per_tile = sr_ref.shape[0] // CHUNK
 
-        def centered(i, carry):
-            tile = i // per_tile
-            start = pl.multiple_of((i % per_tile) * CHUNK, CHUNK)
-            rows = pl.ds(start, CHUNK)
-            signed = jnp.where(tile == 0, sr_ref[rows, :], sc_ref[rows, :])
+        def distances(signed):
             total = None
             for c in range(3):
                 d = jnp.dot(signed, x_ref[c], preferred_element_type=jnp.float32)
                 total = d * d if total is None else total + d * d
-            dist = jnp.sqrt(total).astype(jnp.bfloat16).astype(jnp.float32)
-            later = pltpu.roll(dist, lanes - lag, 1)
-            earlier = jnp.where(first, dist, 0.0)
-            later = jnp.where(first, later, 0.0)
-            mean = (
-                jnp.sum(earlier, axis=1, keepdims=True) + jnp.sum(later, axis=1, keepdims=True)
-            ) / count
-            stack_ref[2 * tile, rows, :] = jnp.where(first, earlier - mean, 0.0).astype(jnp.bfloat16)
-            stack_ref[2 * tile + 1, rows, :] = jnp.where(first, later - mean, 0.0).astype(jnp.bfloat16)
+            dist = jnp.sqrt(total).astype(jnp.bfloat16)
+            sums = jnp.dot(dist, mask_ref[...], preferred_element_type=jnp.float32)
+            mean = (sums[:, 0:1] + sums[:, 1:2]) / count
+            dist = dist.astype(jnp.float32)
+            return dist, pltpu.roll(dist, lanes - lag, 1), mean
+
+        def row_tile(i, carry):
+            rows = pl.ds(pl.multiple_of(i * CHUNK, CHUNK), CHUNK)
+            earlier, later, mean = distances(sr_ref[rows, :])
+            row_ref[rows, :lanes] = jnp.where(first, earlier - mean, 0.0).astype(jnp.bfloat16)
+            row_ref[rows, lanes:] = jnp.where(first, later - mean, 0.0).astype(jnp.bfloat16)
             return carry
 
-        lax.fori_loop(0, 2 * per_tile, centered, 0)
+        def col_tile(i, carry):
+            rows = pl.ds(pl.multiple_of(i * CHUNK, CHUNK), CHUNK)
+            earlier, later, mean = distances(sc_ref[rows, :])
+            zero_lag = (earlier - mean).astype(jnp.bfloat16)
+            lagged = (later - mean).astype(jnp.bfloat16)
+            col_ref[rows, :lanes] = zero_lag
+            col_ref[rows, lanes:] = lagged
+            swap_ref[rows, :lanes] = lagged
+            swap_ref[rows, lanes:] = zero_lag
+            return carry
+
+        lax.fori_loop(0, per_tile, row_tile, 0)
+        lax.fori_loop(0, per_tile, col_tile, 0)
 
     block = inst_ref.shape[0]
     rows = pl.ds(pl.multiple_of(pl.program_id(0) * block, block), block)
     nt = (((1,), (1,)), ((), ()))
-    zero_row = stack_ref[0, rows, :]
-    lag_row = stack_ref[1, rows, :]
-    zero_col = stack_ref[2]
-    lag_col = stack_ref[3]
-    instant = lax.dot_general(zero_row, zero_col, nt, preferred_element_type=jnp.float32)
-    instant = instant + lax.dot_general(lag_row, lag_col, nt, preferred_element_type=jnp.float32)
+    stacked = row_ref[rows, :]
+    instant = lax.dot_general(stacked, col_ref[...], nt, preferred_element_type=jnp.float32)
     inst_ref[...] = (instant / count).astype(inst_ref.dtype)
-    crossed = lax.dot_general(zero_row, lag_col, nt, preferred_element_type=jnp.float32)
-    crossed = crossed + lax.dot_general(lag_row, zero_col, nt, preferred_element_type=jnp.float32)
+    crossed = lax.dot_general(stacked, swap_ref[...], nt, preferred_element_type=jnp.float32)
     cross_ref[...] = (crossed / count).astype(cross_ref.dtype)
 
 
-def covariances(lag, frames, row_signed, col_signed):
+def covariances(lag, frames, mask, row_signed, col_signed):
     lanes = frames.shape[2]
     width = row_signed.shape[0]
     out = jax.ShapeDtypeStruct((width, width), jnp.bfloat16)
@@ -96,6 +100,7 @@
         in_specs=[
             pl.BlockSpec(memory_space=pltpu.SMEM),
             pl.BlockSpec((3, ATOMS, lanes), lambda j: (0, 0, 0)),
+            pl.BlockSpec((lanes, 128), lambda j: (0, 0)),
             pl.BlockSpec((width, ATOMS), lambda j: (0, 0)),
             pl.BlockSpec((width, ATOMS), lambda j: (0, 0)),
         ],
@@ -104,14 +109,25 @@
             pl.BlockSpec((OUT_BLOCK, width), lambda j: (j, 0)),
         ],
         out_shape=[out, out],
-        scratch_shapes=[pltpu.VMEM((4, width, lanes), jnp.bfloat16)],
+        scratch_shapes=[pltpu.VMEM((width, 2 * lanes), jnp.bfloat16)] * 3,
         compiler_params=pltpu.CompilerParams(dimension_semantics=("arbitrary",)),
         cost_estimate=pl.CostEstimate(
             flops=2 * 2 * 3 * width * ATOMS * lanes + 4 * 2 * width * width * lanes,
             transcendentals=2 * width * lanes,
             bytes_accessed=2 * width * width * 2 + 3 * ATOMS * lanes * 2 + 2 * width * ATOMS * 2,
         ),
-    )(lag, frames, row_signed, col_signed)
+    )(lag, frames, mask, row_signed, col_signed)
+
+
+def pair_masks(shift, lanes):
+    pair = jnp.arange(lanes, dtype=jnp.int32)
+    frame = pair % BLOCK_LEN
+    inside = pair < DRAWS * BLOCK_LEN
+    first = inside & (frame < BLOCK_LEN - shift)
+    second = inside & (frame >= shift)
+    column = jnp.arange(128, dtype=jnp.int32)[None, :]
+    mask = jnp.where(column == 0, first[:, None], False) | jnp.where(column == 1, second[:, None], False)
+    return mask.astype(jnp.bfloat16)
 
 
 def signed_pairs(atom_pairs, first_feature, width):
@@ -133,7 +149,8 @@
     frames = jnp.pad(frames, ((0, 0), (0, 0), (0, lanes - pairs)))
     row_signed = signed_pairs(atom_pairs, lax.axis_index("row") * width, width)
     col_signed = signed_pairs(atom_pairs, lax.axis_index("col") * width, width)
-    instant, crossed = covariances(lag_time, frames, row_signed, col_signed)
+    mask = pair_masks(lag_time[0], lanes)
+    instant, crossed = covariances(lag_time, frames, mask, row_signed, col_signed)
     return (instant[None], crossed[None])
 
 

time: 77.6 us -> 79.2 us (1.021)
  Pallas kernels: 19.2 us -> 20.8 us
  waiting for transfers between devices: 21 us -> 20 us
  other arithmetic: 4.2 us -> 5.18 us
    all_to_all x1, waiting for transfers between devices: 14.4 us -> 12.7 us  [gather_blocks(): every = lax.all_to_all(spread, 'rep', 0, 0, tiled=True)]
    pallas_call x1, Pallas kernels: 19.2 us -> 20.8 us  [covariances(): pl.pallas_call(covariance_kernel, grid=(width // OUT_BLOCK,), in_specs=[p...]
    convert_element_type x0 -> x1, other arithmetic: none -> 0.96 us  [pair_masks(): return mask.astype(jnp.bfloat16)]
  transfers between devices with their start and end apart: 2 -> 2, of which waited for: 2 -> 2; matrix products, arithmetic and copies ran while one was open for 8% -> 9% of each run, Pallas kernels for 0% -> 0%
where the time goes in v6:
time: 79.2 us; the launch traced here: 78 us
  starting transfers between devices  23.5 us (30%)
  Pallas kernels  20.8 us (26%)
  waiting for transfers between devices  20 us (25%)
  local copies, waits for them, and re-layouts  7.14 us (9%)
  other arithmetic  5.18 us (7%)
  between operations  1.38 us (2%)
    pallas_call x1, Pallas kernels, covariances(): pl.pallas_call(covariance_kernel, grid=(width // OUT_BLOCK,), in_specs=[p...  20.8 us
    all_to_all x1, starting transfers between devices, gather_blocks(): every = lax.all_to_all(spread, 'rep', 0, 0, tiled=True)  16.7 us
    all_to_all x1, waiting for transfers between devices, gather_blocks(): every = lax.all_to_all(spread, 'rep', 0, 0, tiled=True)  12.7 us
    all_to_all x1, waiting for transfers between devices, gather_blocks(): parts = lax.all_to_all(spread, ('row', 'col'), 0, 0, tiled=True)  7.22 us
    all_to_all x1, starting transfers between devices, gather_blocks(): parts = lax.all_to_all(spread, ('row', 'col'), 0, 0, tiled=True)  6.75 us
    convert_element_type x2, other arithmetic, signed_pairs(): return ((first_atoms[:, None] == atom_ids).astype(jnp.float32) - (second_...  2.09 us
  transfers between devices with their start and end apart: 2, of which 2 were waited for; matrix products, arithmetic and copies ran while one was open for 9% of the time, Pallas kernels for 0%

profile of v6, /device:TPU:1, one launch (start us, length us, event | category | flops | bytes accessed | tf_op | source)
XLA Modules:
  0.0 78.0 jit_solution(3837275017179579806)
XLA Ops:
  0.6 0.0 copy-start
  0.7 0.9 %copy-done = bf16[4,32,3,128]{3,1,2,0:T(8,128)(2,1)S(1)} copy-done((bf16[4,32,3,128]{3,1,2,0:T(8,128)(2,1)S(1)}, bf16[4,32,3,128]{3,1,2,0:T(8,128)(2,1)}, u32[]{:S(2)}) %copy-start) | copy-done | bytes 98328
  1.5 0.8 %broadcast_in_dim.71 = bf16[32,4,2,3,128]{4,2,3,1,0:T(2,128)(2,1)} broadcast(bf16[4,2,3,128]{3,1,2,0:T(2,128)(2,1)S(1)} %constant_dynamic-slice_fusion.4), dimensions={1,2,3,4} | broadcast | bytes 202752 | tf_op jit(solution)/shard_map/broadcast_in_dim | solution.py:28
  2.3 16.7 %all-to-all-start = ((bf16[32,4,2,3,128]{4,2,3,1,0:T(2,128)(2,1)}), bf16[32,4,2,3,128]{4,2,3,1,0:T(2,128)(2,1)S(1)}, u32[]{:S(2)}, u32[]{:S(2)}) async-start(bf16[32,4,2,3,128]{4,2,3,1,0:T(2,128)(2,1)} %broadcast_in_dim.71), calls=%async_computation | async-start | bytes 393216 | tf_op jit(solution)/shard_map/all_to_all | solution.py:29
  19.1 0.7 fusion.8
  19.8 1.4 %gather_fusion = s32[22]{0:T(128)S(1)} fusion(s32[128]{0:T(128)} %param.7, s32[1024]{0:T(1024)S(1)} %pad_clamp_fusion.1), kind=kCustom, calls=%fused_computation | custom fusion | bytes 264 | tf_op jit(solution)/shard_map/jit(_take)/gather | solution.py:31
  21.1 0.7 compare_and_fusion
  21.8 0.7 fusion.7
  23.1 1.0 %or_convert_fusion.mask_ref = bf16[768,128]{1,0:T(8,128)(2,1)} fusion(pred[128]{0:T(512)(128)(4,1)S(1)} %get-tuple-element.14, pred[128]{0:T(512)(128)(4,1)S(1)} %get-tuple-element.15, pred[768]{0:T(1024)(128)(4,1)S(1)} %get-tuple-element.12, pred[768]{0:T(1024)(128)(4,1)S(1)} %get-tuple-element.13), kind=kLoop, calls=%fused_computation.8 | loop fusion | flops 393216 | bytes 198400 | tf_op jit(solution)/shard_map/convert_element_type | solution.py:130
  24.1 0.9 %fusion.9 = (s32[1,4096]{1,0:T(1,128)S(1)}, s32[1,4096]{1,0:T(1,128)S(1)}) fusion(s32[2,4096]{1,0:T(2,128)} %param.9), kind=kLoop, calls=%fused_computation.38 | loop fusion | bytes 65536 | tf_op jit(solution)/shard_map/slice | solution.py:134
  25.0 12.7 %all-to-all-done = bf16[32,4,2,3,128]{4,2,3,1,0:T(2,128)(2,1)S(1)} async-done(((bf16[32,4,2,3,128]{4,2,3,1,0:T(2,128)(2,1)}), bf16[32,4,2,3,128]{4,2,3,1,0:T(2,128)(2,1)S(1)}, u32[]{:S(2)}, u32[]{:S(2)}) %all-to-all-start) | async-done | bytes 196640 | tf_op jit(solution)/shard_map/all_to_all | solution.py:29
  37.7 0.6 gather_fusion.1
  38.3 0.1 broadcast_select_fusion
  38.4 1.1 %broadcast_in_dim.73 = bf16[16,22,2,3,128]{4,2,3,1,0:T(2,128)(2,1)} broadcast(bf16[22,2,3,128]{3,1,2,0:T(2,128)(2,1)S(1)} %broadcast_select_fusion), dimensions={1,2,3,4} | broadcast | bytes 574464 | tf_op jit(solution)/shard_map/broadcast_in_dim | solution.py:35
  39.5 6.8 %all-to-all-start.1 = ((bf16[16,22,2,3,128]{4,2,3,1,0:T(2,128)(2,1)}), bf16[16,22,2,3,128]{4,2,3,1,0:T(2,128)(2,1)S(1)}, u32[]{:S(2)}, u32[]{:S(2)}) async-start(bf16[16,22,2,3,128]{4,2,3,1,0:T(2,128)(2,1)} %broadcast_in_dim.73), calls=%async_computation.1 | async-start | bytes 1081344 | tf_op jit(solution)/shard_map/all_to_all | solution.py:36
  46.3 1.0 %subtract_convert_fusion.1.sr_ref = bf16[1024,128]{1,0:T(8,128)(2,1)} fusion(s32[1024]{0:T(1024)S(1)} %bitcast.39, s32[1024]{0:T(1024)S(1)} %bitcast.40), kind=kLoop, calls=%fused_computation.5 | loop fusion | flops 786432 | bytes 270336 | tf_op jit(solution)/shard_map/convert_element_type | solution.py:140
  47.4 1.1 %subtract_convert_fusion.sc_ref = bf16[1024,128]{1,0:T(8,128)(2,1)} fusion(s32[1024]{0:T(1024)S(1)} %bitcast.37, s32[1024]{0:T(1024)S(1)} %bitcast.38), kind=kLoop, calls=%fused_computation.2 | loop fusion | flops 786432 | bytes 270336 | tf_op jit(solution)/shard_map/convert_element_type | solution.py:140
  48.4 7.2 %all-to-all-done.1 = bf16[16,22,2,3,128]{4,2,3,1,0:T(2,128)(2,1)S(1)} async-done(((bf16[16,22,2,3,128]{4,2,3,1,0:T(2,128)(2,1)}), bf16[16,22,2,3,128]{4,2,3,1,0:T(2,128)(2,1)S(1)}, u32[]{:S(2)}, u32[]{:S(2)}) %all-to-all-start.1) | async-done | bytes 540704 | tf_op jit(solution)/shard_map/all_to_all | solution.py:36
  55.6 0.4 copy.10
  56.1 0.2 copy.12
  56.3 0.9 %pad.4.x_ref = bf16[3,128,768]{2,1,0:T(8,128)(2,1)} pad(bf16[3,128,704]{2,1,0:T(8,128)(2,1)S(1)} %copy.12, bf16[]{:T(256)} %constant.66.clone.1), padding=0_0x0_0x0_64 | pad | bytes 1130498 | tf_op jit(solution)/shard_map/jit(_pad)/pad | solution.py:149
  57.2 20.8 %shard_map.68 = (bf16[1024,1024]{1,0:T(8,128)(2,1)}, bf16[1024,1024]{1,0:T(8,128)(2,1)}) custom-call(s32[1]{0:T(128)} %copy.13.lag_ref, bf16[3,128,768]{2,1,0:T(8,128)(2,1)} %pad.4.x_ref, bf16[768,128]{1,0:T(8,128)(2,1)} %or_convert_fusion.mask_ref, bf16[1024,128]{1,0:T(8,128)(2,1)} %subtract_convert_fusion.1.sr_ref, ...), custom_call_target="tpu_custom_call" | custom-call | flops 7650410496 | bytes 5308416 | tf_op jit(solution)/shard_map/pallas_call | solution.py:97
  (7 shorter events, 0.1 us)
Async XLA Ops:
  0.6 0.9 %copy-start = (bf16[4,32,3,128]{3,1,2,0:T(8,128)(2,1)S(1)}, bf16[4,32,3,128]{3,1,2,0:T(8,128)(2,1)}, u32[]{:S(2)}) copy-start(bf16[4,32,3,128]{3,1,2,0:T(8,128)(2,1)} %param.5) | copy-start | bytes 294916
  2.3 35.4 %all-to-all-start = ((bf16[32,4,2,3,128]{4,2,3,1,0:T(2,128)(2,1)}), bf16[32,4,2,3,128]{4,2,3,1,0:T(2,128)(2,1)S(1)}, u32[]{:S(2)}, u32[]{:S(2)}) async-start(bf16[32,4,2,3,128]{4,2,3,1,0:T(2,128)(2,1)} %broadcast_in_dim.71), calls=%async_computation | async-start | bytes 393216 | tf_op jit(solution)/shard_map/all_to_all | solution.py:29
  39.5 16.1 %all-to-all-start.1 = ((bf16[16,22,2,3,128]{4,2,3,1,0:T(2,128)(2,1)}), bf16[16,22,2,3,128]{4,2,3,1,0:T(2,128)(2,1)S(1)}, u32[]{:S(2)}, u32[]{:S(2)}) async-start(bf16[16,22,2,3,128]{4,2,3,1,0:T(2,128)(2,1)} %broadcast_in_dim.73), calls=%async_computation.1 | async-start | bytes 1081344 | tf_op jit(solution)/shard_map/all_to_all | solution.py:36

commit v7 on v5

--- a/solution.py
+++ b/solution.py
@@ -11,8 +11,7 @@
 ATOMS = 128
 BLOCK_LEN = 32
 DRAWS = 22
-CHUNK = 128
-OUT_BLOCK = 256
+OUT_BLOCK = 1024
 
 
 def gather_blocks(coordinates, resample, block_slot):
@@ -47,13 +46,8 @@
         pair = lax.broadcasted_iota(jnp.int32, (1, lanes), 1)
         first = ((pair % BLOCK_LEN) < (BLOCK_LEN - lag)) & (pair < DRAWS * BLOCK_LEN)
 
-        per_tile = sr_ref.shape[0] // CHUNK
-
-        def centered(i, carry):
-            tile = i // per_tile
-            start = pl.multiple_of((i % per_tile) * CHUNK, CHUNK)
-            rows = pl.ds(start, CHUNK)
-            signed = jnp.where(tile == 0, sr_ref[rows, :], sc_ref[rows, :])
+        for tile, signed_ref in enumerate((sr_ref, sc_ref)):
+            signed = signed_ref[...]
             total = None
             for c in range(3):
                 d = jnp.dot(signed, x_ref[c], preferred_element_type=jnp.float32)
@@ -65,11 +59,8 @@
             mean = (
                 jnp.sum(earlier, axis=1, keepdims=True) + jnp.sum(later, axis=1, keepdims=True)
             ) / count
-            stack_ref[2 * tile, rows, :] = jnp.where(first, earlier - mean, 0.0).astype(jnp.bfloat16)
-            stack_ref[2 * tile + 1, rows, :] = jnp.where(first, later - mean, 0.0).astype(jnp.bfloat16)
-            return carry
-
-        lax.fori_loop(0, 2 * per_tile, centered, 0)
+            stack_ref[2 * tile] = jnp.where(first, earlier - mean, 0.0).astype(jnp.bfloat16)
+            stack_ref[2 * tile + 1] = jnp.where(first, later - mean, 0.0).astype(jnp.bfloat16)
 
     block = inst_ref.shape[0]
     rows = pl.ds(pl.multiple_of(pl.program_id(0) * block, block), block)
@@ -92,7 +83,7 @@
     out = jax.ShapeDtypeStruct((width, width), jnp.bfloat16)
     return pl.pallas_call(
         covariance_kernel,
-        grid=(width // OUT_BLOCK,),
+        grid=(pl.cdiv(width, OUT_BLOCK),),
         in_specs=[
             pl.BlockSpec(memory_space=pltpu.SMEM),
             pl.BlockSpec((3, ATOMS, lanes), lambda j: (0, 0, 0)),
@@ -100,8 +91,8 @@
             pl.BlockSpec((width, ATOMS), lambda j: (0, 0)),
         ],
         out_specs=[
-            pl.BlockSpec((OUT_BLOCK, width), lambda j: (j, 0)),
-            pl.BlockSpec((OUT_BLOCK, width), lambda j: (j, 0)),
+            pl.BlockSpec((min(OUT_BLOCK, width), width), lambda j: (j, 0)),
+            pl.BlockSpec((min(OUT_BLOCK, width), width), lambda j: (j, 0)),
         ],
         out_shape=[out, out],
         scratch_shapes=[pltpu.VMEM((4, width, lanes), jnp.bfloat16)],

time: 77.6 us -> 74.1 us (0.955)
  Pallas kernels: 19.2 us -> 15.7 us
    pallas_call x1, Pallas kernels: 19.2 us -> 15.7 us  [covariances(): pl.pallas_call(covariance_kernel, grid=(pl.cdiv(width, OUT_BLOCK),), in_s...]
  transfers between devices with their start and end apart: 2 -> 2, of which waited for: 2 -> 2; matrix products, arithmetic and copies ran while one was open for 8% -> 9% of each run, Pallas kernels for 0% -> 0%
where the time goes in v7:
time: 74.1 us; the launch traced here: 72.9 us
  starting transfers between devices  23.5 us (32%)
  waiting for transfers between devices  21 us (28%)
  Pallas kernels  15.7 us (21%)
  local copies, waits for them, and re-layouts  7.13 us (10%)
  other arithmetic  4.2 us (6%)
  between operations  1.36 us (2%)
    all_to_all x1, starting transfers between devices, gather_blocks(): every = lax.all_to_all(spread, 'rep', 0, 0, tiled=True)  16.7 us
    pallas_call x1, Pallas kernels, covariances(): pl.pallas_call(covariance_kernel, grid=(pl.cdiv(width, OUT_BLOCK),), in_s...  15.7 us
    all_to_all x1, waiting for transfers between devices, gather_blocks(): every = lax.all_to_all(spread, 'rep', 0, 0, tiled=True)  14.4 us
    all_to_all x1, starting transfers between devices, gather_blocks(): parts = lax.all_to_all(spread, ('row', 'col'), 0, 0, tiled=True)  6.75 us
    all_to_all x1, waiting for transfers between devices, gather_blocks(): parts = lax.all_to_all(spread, ('row', 'col'), 0, 0, tiled=True)  6.59 us
    convert_element_type x2, other arithmetic, signed_pairs(): return ((first_atoms[:, None] == atom_ids).astype(jnp.float32) - (second_...  2.08 us
  transfers between devices with their start and end apart: 2, of which 2 were waited for; matrix products, arithmetic and copies ran while one was open for 9% of the time, Pallas kernels for 0%

profile of v7, /device:TPU:1, one launch (start us, length us, event | category | flops | bytes accessed | tf_op | source)
XLA Modules:
  0.0 72.9 jit_solution(7125615235713603784)
XLA Ops:
  0.6 0.0 copy-start
  0.7 0.9 %copy-done = bf16[4,32,3,128]{3,1,2,0:T(8,128)(2,1)S(1)} copy-done((bf16[4,32,3,128]{3,1,2,0:T(8,128)(2,1)S(1)}, bf16[4,32,3,128]{3,1,2,0:T(8,128)(2,1)}, u32[]{:S(2)}) %copy-start) | copy-done | bytes 98328
  1.5 0.8 %broadcast_in_dim.21 = bf16[32,4,2,3,128]{4,2,3,1,0:T(2,128)(2,1)} broadcast(bf16[4,2,3,128]{3,1,2,0:T(2,128)(2,1)S(1)} %constant_dynamic-slice_fusion.4), dimensions={1,2,3,4} | broadcast | bytes 202752 | tf_op jit(solution)/shard_map/broadcast_in_dim | solution.py:27
  2.3 16.7 %all-to-all-start = ((bf16[32,4,2,3,128]{4,2,3,1,0:T(2,128)(2,1)}), bf16[32,4,2,3,128]{4,2,3,1,0:T(2,128)(2,1)S(1)}, u32[]{:S(2)}, u32[]{:S(2)}) async-start(bf16[32,4,2,3,128]{4,2,3,1,0:T(2,128)(2,1)} %broadcast_in_dim.21), calls=%async_computation | async-start | bytes 393216 | tf_op jit(solution)/shard_map/all_to_all | solution.py:28
  19.1 0.7 fusion.1
  19.8 1.4 %gather_fusion = s32[22]{0:T(128)S(1)} fusion(s32[128]{0:T(128)} %param.7, s32[1024]{0:T(1024)S(1)} %pad_clamp_fusion.1), kind=kCustom, calls=%fused_computation | custom fusion | bytes 264 | tf_op jit(solution)/shard_map/jit(_take)/gather | solution.py:30
  21.1 0.7 compare_and_fusion
  21.8 0.7 fusion
  22.5 0.9 %fusion.2 = (s32[1,4096]{1,0:T(1,128)S(1)}, s32[1,4096]{1,0:T(1,128)S(1)}) fusion(s32[2,4096]{1,0:T(2,128)} %param.9), kind=kLoop, calls=%fused_computation.25 | loop fusion | bytes 65536 | tf_op jit(solution)/shard_map/slice | solution.py:109
  23.3 14.4 %all-to-all-done = bf16[32,4,2,3,128]{4,2,3,1,0:T(2,128)(2,1)S(1)} async-done(((bf16[32,4,2,3,128]{4,2,3,1,0:T(2,128)(2,1)}), bf16[32,4,2,3,128]{4,2,3,1,0:T(2,128)(2,1)S(1)}, u32[]{:S(2)}, u32[]{:S(2)}) %all-to-all-start) | async-done | bytes 196640 | tf_op jit(solution)/shard_map/all_to_all | solution.py:28
  37.7 0.6 gather_fusion.1
  38.3 0.1 broadcast_select_fusion
  38.4 1.1 %broadcast_in_dim.23 = bf16[16,22,2,3,128]{4,2,3,1,0:T(2,128)(2,1)} broadcast(bf16[22,2,3,128]{3,1,2,0:T(2,128)(2,1)S(1)} %broadcast_select_fusion), dimensions={1,2,3,4} | broadcast | bytes 574464 | tf_op jit(solution)/shard_map/broadcast_in_dim | solution.py:34
  39.5 6.8 %all-to-all-start.1 = ((bf16[16,22,2,3,128]{4,2,3,1,0:T(2,128)(2,1)}), bf16[16,22,2,3,128]{4,2,3,1,0:T(2,128)(2,1)S(1)}, u32[]{:S(2)}, u32[]{:S(2)}) async-start(bf16[16,22,2,3,128]{4,2,3,1,0:T(2,128)(2,1)} %broadcast_in_dim.23), calls=%async_computation.1 | async-start | bytes 1081344 | tf_op jit(solution)/shard_map/all_to_all | solution.py:35
  47.0 1.0 %subtract_convert_fusion.1.sr_ref = bf16[1024,128]{1,0:T(8,128)(2,1)} fusion(s32[1024]{0:T(1024)S(1)} %bitcast.36, s32[1024]{0:T(1024)S(1)} %bitcast.37), kind=kLoop, calls=%fused_computation.5 | loop fusion | flops 786432 | bytes 270336 | tf_op jit(solution)/shard_map/convert_element_type | solution.py:115
  48.0 1.0 %subtract_convert_fusion.sc_ref = bf16[1024,128]{1,0:T(8,128)(2,1)} fusion(s32[1024]{0:T(1024)S(1)} %bitcast.34, s32[1024]{0:T(1024)S(1)} %bitcast.35), kind=kLoop, calls=%fused_computation.2 | loop fusion | flops 786432 | bytes 270336 | tf_op jit(solution)/shard_map/convert_element_type | solution.py:115
  49.0 6.6 %all-to-all-done.1 = bf16[16,22,2,3,128]{4,2,3,1,0:T(2,128)(2,1)S(1)} async-done(((bf16[16,22,2,3,128]{4,2,3,1,0:T(2,128)(2,1)}), bf16[16,22,2,3,128]{4,2,3,1,0:T(2,128)(2,1)S(1)}, u32[]{:S(2)}, u32[]{:S(2)}) %all-to-all-start.1) | async-done | bytes 540704 | tf_op jit(solution)/shard_map/all_to_all | solution.py:35
  55.6 0.4 copy.10
  56.1 0.2 copy.12
  56.3 0.9 %pad.4.x_ref = bf16[3,128,768]{2,1,0:T(8,128)(2,1)} pad(bf16[3,128,704]{2,1,0:T(8,128)(2,1)S(1)} %copy.12, bf16[]{:T(256)} %constant.50.clone.1), padding=0_0x0_0x0_64 | pad | bytes 1130498 | tf_op jit(solution)/shard_map/jit(_pad)/pad | solution.py:124
  57.2 15.7 %shard_map.68 = (bf16[1024,1024]{1,0:T(8,128)(2,1)}, bf16[1024,1024]{1,0:T(8,128)(2,1)}) custom-call(s32[1]{0:T(128)S(6)} %copy.13.lag_ref, bf16[3,128,768]{2,1,0:T(8,128)(2,1)} %pad.4.x_ref, bf16[1024,128]{1,0:T(8,128)(2,1)} %subtract_convert_fusion.1.sr_ref, bf16[1024,128]{1,0:T(8,128)(2,1)} %subtract_convert_fusion.sc_ref), custom_call_target="tpu_custom_call" | custom-call | flops 7650410496 | bytes 5308416 | tf_op jit(solution)/shard_map/pallas_call | solution.py:84
  (5 shorter events, 0.1 us)
Async XLA Ops:
  0.6 0.9 %copy-start = (bf16[4,32,3,128]{3,1,2,0:T(8,128)(2,1)S(1)}, bf16[4,32,3,128]{3,1,2,0:T(8,128)(2,1)}, u32[]{:S(2)}) copy-start(bf16[4,32,3,128]{3,1,2,0:T(8,128)(2,1)} %param.5) | copy-start | bytes 294916
  2.3 35.4 %all-to-all-start = ((bf16[32,4,2,3,128]{4,2,3,1,0:T(2,128)(2,1)}), bf16[32,4,2,3,128]{4,2,3,1,0:T(2,128)(2,1)S(1)}, u32[]{:S(2)}, u32[]{:S(2)}) async-start(bf16[32,4,2,3,128]{4,2,3,1,0:T(2,128)(2,1)} %broadcast_in_dim.21), calls=%async_computation | async-start | bytes 393216 | tf_op jit(solution)/shard_map/all_to_all | solution.py:28
  39.5 16.1 %all-to-all-start.1 = ((bf16[16,22,2,3,128]{4,2,3,1,0:T(2,128)(2,1)}), bf16[16,22,2,3,128]{4,2,3,1,0:T(2,128)(2,1)S(1)}, u32[]{:S(2)}, u32[]{:S(2)}) async-start(bf16[16,22,2,3,128]{4,2,3,1,0:T(2,128)(2,1)} %broadcast_in_dim.23), calls=%async_computation.1 | async-start | bytes 1081344 | tf_op jit(solution)/shard_map/all_to_all | solution.py:35

commit v8 on v7

--- a/solution.py
+++ b/solution.py
@@ -22,17 +22,20 @@
     member = lax.axis_index("row") * lax.axis_size("col") + lax.axis_index("col")
     if groups == 1:
         member = 0
-    piece = lax.dynamic_slice_in_dim(coordinates, member * frames, frames, axis=1)
+    flat = coordinates.reshape(coordinates.shape[0], BLOCK_LEN, 3 * ATOMS)
+    piece = lax.dynamic_slice_in_dim(flat, member * frames, frames, axis=1)
+    piece = piece.reshape(piece.shape[0], frames * 3 * ATOMS)
     reps = lax.axis_size("rep")
     spread = jnp.broadcast_to(piece[None], (reps,) + piece.shape)
     every = lax.all_to_all(spread, "rep", 0, 0, tiled=True)
-    every = every.reshape((-1,) + piece.shape[1:])
+    every = every.reshape(-1, piece.shape[1])
     slots = jnp.take(block_slot, resample[0], axis=0)
     picked = jnp.take(every, slots, axis=0)
     if groups == 1:
-        return picked
+        return picked.reshape(DRAWS, BLOCK_LEN, 3, ATOMS)
     spread = jnp.broadcast_to(picked[None], (groups,) + picked.shape)
     parts = lax.all_to_all(spread, ("row", "col"), 0, 0, tiled=True)
+    parts = parts.reshape(groups, DRAWS, frames, 3, ATOMS)
     return jnp.swapaxes(parts, 0, 1).reshape(DRAWS, BLOCK_LEN, 3, ATOMS)
 
 

time: 74.1 us -> 74.8 us (level)
  the two profiles are of different devices: /device:TPU:1 before, /device:TPU:8 now
where the time goes in v8:
time: 74.8 us; the launch traced here: 74.3 us
  starting transfers between devices  22.9 us (31%)
  waiting for transfers between devices  22.9 us (31%)
  Pallas kernels  15.7 us (21%)
  local copies, waits for them, and re-layouts  7.31 us (10%)
  other arithmetic  4.17 us (6%)
  between operations  1.38 us (2%)
    all_to_all x1, waiting for transfers between devices, gather_blocks(): every = lax.all_to_all(spread, 'rep', 0, 0, tiled=True)  15.8 us
    pallas_call x1, Pallas kernels, covariances(): pl.pallas_call(covariance_kernel, grid=(pl.cdiv(width, OUT_BLOCK),), in_s...  15.7 us
    all_to_all x1, starting transfers between devices, gather_blocks(): every = lax.all_to_all(spread, 'rep', 0, 0, tiled=True)  15.5 us
    all_to_all x1, starting transfers between devices, gather_blocks(): parts = lax.all_to_all(spread, ('row', 'col'), 0, 0, tiled=True)  7.39 us
    all_to_all x1, waiting for transfers between devices, gather_blocks(): parts = lax.all_to_all(spread, ('row', 'col'), 0, 0, tiled=True)  7.12 us
    convert_element_type x2, other arithmetic, signed_pairs(): return ((first_atoms[:, None] == atom_ids).astype(jnp.float32) - (second_...  2.08 us
  transfers between devices with their start and end apart: 2, of which 2 were waited for; matrix products, arithmetic and copies ran while one was open for 8% of the time, Pallas kernels for 0%

profile of v8, /device:TPU:8, one launch (start us, length us, event | category | flops | bytes accessed | tf_op | source)
XLA Modules:
  0.0 74.3 jit_solution(18377780003780946516)
XLA Ops:
  0.6 0.0 copy-start
  0.7 0.9 %copy-done = bf16[4,32,3,128]{3,1,2,0:T(8,128)(2,1)S(1)} copy-done((bf16[4,32,3,128]{3,1,2,0:T(8,128)(2,1)S(1)}, bf16[4,32,3,128]{3,1,2,0:T(8,128)(2,1)}, u32[]{:S(2)}) %copy-start) | copy-done | bytes 98328
  1.6 0.7 broadcast_in_dim.39
  2.3 15.5 %all-to-all-start = ((bf16[32,4,768]{2,1,0:T(4,128)(2,1)}), bf16[32,4,768]{2,1,0:T(4,128)(2,1)S(1)}, u32[]{:S(2)}, u32[]{:S(2)}) async-start(bf16[32,4,768]{2,1,0:T(4,128)(2,1)} %broadcast_in_dim.39), calls=%async_computation | async-start | bytes 393216 | tf_op jit(solution)/shard_map/all_to_all | solution.py:30
  17.8 0.7 fusion.1
  18.5 1.4 %gather_fusion = s32[22]{0:T(128)S(1)} fusion(s32[128]{0:T(128)} %param.7, s32[1024]{0:T(1024)S(1)} %pad_clamp_fusion.1), kind=kCustom, calls=%fused_computation | custom fusion | bytes 264 | tf_op jit(solution)/shard_map/jit(_take)/gather | solution.py:32
  19.8 0.7 compare_and_fusion
  20.5 0.7 fusion
  21.2 0.9 %fusion.2 = (s32[1,4096]{1,0:T(1,128)S(1)}, s32[1,4096]{1,0:T(1,128)S(1)}) fusion(s32[2,4096]{1,0:T(2,128)} %param.9), kind=kLoop, calls=%fused_computation.26 | loop fusion | bytes 65536 | tf_op jit(solution)/shard_map/slice | solution.py:112
  22.0 15.8 %all-to-all-done = bf16[32,4,768]{2,1,0:T(4,128)(2,1)S(1)} async-done(((bf16[32,4,768]{2,1,0:T(4,128)(2,1)}), bf16[32,4,768]{2,1,0:T(4,128)(2,1)S(1)}, u32[]{:S(2)}, u32[]{:S(2)}) %all-to-all-start) | async-done | bytes 196640 | tf_op jit(solution)/shard_map/all_to_all | solution.py:30
  37.8 0.1 reshape.121
  37.9 0.6 gather_fusion.1
  38.5 0.1 broadcast_select_fusion
  38.6 0.9 %broadcast_in_dim.41 = bf16[16,22,768]{2,1,0:T(8,128)(2,1)} broadcast(bf16[22,768]{1,0:T(8,128)(2,1)S(1)} %broadcast_select_fusion), dimensions={1,2} | broadcast | bytes 574464 | tf_op jit(solution)/shard_map/broadcast_in_dim | solution.py:36
  39.4 7.4 %all-to-all-start.1 = ((bf16[16,22,768]{2,1,0:T(8,128)(2,1)}), bf16[16,22,768]{2,1,0:T(8,128)(2,1)S(1)}, u32[]{:S(2)}, u32[]{:S(2)}) async-start(bf16[16,22,768]{2,1,0:T(8,128)(2,1)} %broadcast_in_dim.41), calls=%async_computation.1 | async-start | bytes 1179648 | tf_op jit(solution)/shard_map/all_to_all | solution.py:37
  47.5 1.0 %subtract_convert_fusion.1.sr_ref = bf16[1024,128]{1,0:T(8,128)(2,1)} fusion(s32[1024]{0:T(1024)S(1)} %bitcast.45, s32[1024]{0:T(1024)S(1)} %bitcast.46), kind=kLoop, calls=%fused_computation.5 | loop fusion | flops 786432 | bytes 270336 | tf_op jit(solution)/shard_map/convert_element_type | solution.py:118
  48.5 1.0 %subtract_convert_fusion.sc_ref = bf16[1024,128]{1,0:T(8,128)(2,1)} fusion(s32[1024]{0:T(1024)S(1)} %bitcast.43, s32[1024]{0:T(1024)S(1)} %bitcast.44), kind=kLoop, calls=%fused_computation.2 | loop fusion | flops 786432 | bytes 270336 | tf_op jit(solution)/shard_map/convert_element_type | solution.py:118
  49.6 7.1 %all-to-all-done.1 = bf16[16,22,768]{2,1,0:T(8,128)(2,1)S(1)} async-done(((bf16[16,22,768]{2,1,0:T(8,128)(2,1)}), bf16[16,22,768]{2,1,0:T(8,128)(2,1)S(1)}, u32[]{:S(2)}, u32[]{:S(2)}) %all-to-all-start.1) | async-done | bytes 540704 | tf_op jit(solution)/shard_map/all_to_all | solution.py:37
  56.7 0.1 copy.12
  56.8 0.2 reshape.122
  57.0 0.5 copy.13
  57.5 0.2 copy.15
  57.8 0.9 %pad.4.x_ref = bf16[3,128,768]{2,1,0:T(8,128)(2,1)} pad(bf16[3,128,704]{2,1,0:T(8,128)(2,1)S(1)} %copy.15, bf16[]{:T(256)} %constant.50.clone.1), padding=0_0x0_0x0_64 | pad | bytes 1130498 | tf_op jit(solution)/shard_map/jit(_pad)/pad | solution.py:127
  58.6 15.7 %shard_map.68 = (bf16[1024,1024]{1,0:T(8,128)(2,1)}, bf16[1024,1024]{1,0:T(8,128)(2,1)}) custom-call(s32[1]{0:T(128)S(6)} %copy.19.lag_ref, bf16[3,128,768]{2,1,0:T(8,128)(2,1)} %pad.4.x_ref, bf16[1024,128]{1,0:T(8,128)(2,1)} %subtract_convert_fusion.1.sr_ref, bf16[1024,128]{1,0:T(8,128)(2,1)} %subtract_convert_fusion.sc_ref), custom_call_target="tpu_custom_call" | custom-call | flops 7650410496 | bytes 5308416 | tf_op jit(solution)/shard_map/pallas_call | solution.py:87
  (7 shorter events, 0.1 us)
Async XLA Ops:
  0.6 0.9 %copy-start = (bf16[4,32,3,128]{3,1,2,0:T(8,128)(2,1)S(1)}, bf16[4,32,3,128]{3,1,2,0:T(8,128)(2,1)}, u32[]{:S(2)}) copy-start(bf16[4,32,3,128]{3,1,2,0:T(8,128)(2,1)} %param.5) | copy-start | bytes 294916
  2.3 35.5 %all-to-all-start = ((bf16[32,4,768]{2,1,0:T(4,128)(2,1)}), bf16[32,4,768]{2,1,0:T(4,128)(2,1)S(1)}, u32[]{:S(2)}, u32[]{:S(2)}) async-start(bf16[32,4,768]{2,1,0:T(4,128)(2,1)} %broadcast_in_dim.39), calls=%async_computation | async-start | bytes 393216 | tf_op jit(solution)/shard_map/all_to_all | solution.py:30
  39.4 17.3 %all-to-all-start.1 = ((bf16[16,22,768]{2,1,0:T(8,128)(2,1)}), bf16[16,22,768]{2,1,0:T(8,128)(2,1)S(1)}, u32[]{:S(2)}, u32[]{:S(2)}) async-start(bf16[16,22,768]{2,1,0:T(8,128)(2,1)} %broadcast_in_dim.41), calls=%async_computation.1 | async-start | bytes 1179648 | tf_op jit(solution)/shard_map/all_to_all | solution.py:37

commit v9 on v7

--- a/solution.py
+++ b/solution.py
@@ -36,13 +36,16 @@
     return jnp.swapaxes(parts, 0, 1).reshape(DRAWS, BLOCK_LEN, 3, ATOMS)
 
 
-def covariance_kernel(lag_ref, x_ref, sr_ref, sc_ref, inst_ref, cross_ref, stack_ref):
+def covariance_kernel(lag_ref, raw_ref, sr_ref, sc_ref, inst_ref, cross_ref, stack_ref, x_ref):
     lag = lag_ref[0]
     lanes = x_ref.shape[2]
+    pairs = raw_ref.shape[2]
     count = (2 * DRAWS * (BLOCK_LEN - lag)).astype(jnp.float32)
 
     @pl.when(pl.program_id(0) == 0)
     def _():
+        x_ref[:, :, pairs:] = jnp.zeros((3, ATOMS, lanes - pairs), x_ref.dtype)
+        x_ref[:, :, :pairs] = raw_ref[...]
         pair = lax.broadcasted_iota(jnp.int32, (1, lanes), 1)
         first = ((pair % BLOCK_LEN) < (BLOCK_LEN - lag)) & (pair < DRAWS * BLOCK_LEN)
 
@@ -78,7 +81,8 @@
 
 
 def covariances(lag, frames, row_signed, col_signed):
-    lanes = frames.shape[2]
+    pairs = frames.shape[2]
+    lanes = -(-pairs // 128) * 128
     width = row_signed.shape[0]
     out = jax.ShapeDtypeStruct((width, width), jnp.bfloat16)
     return pl.pallas_call(
@@ -86,7 +90,7 @@
         grid=(pl.cdiv(width, OUT_BLOCK),),
         in_specs=[
             pl.BlockSpec(memory_space=pltpu.SMEM),
-            pl.BlockSpec((3, ATOMS, lanes), lambda j: (0, 0, 0)),
+            pl.BlockSpec((3, ATOMS, pairs), lambda j: (0, 0, 0)),
             pl.BlockSpec((width, ATOMS), lambda j: (0, 0)),
             pl.BlockSpec((width, ATOMS), lambda j: (0, 0)),
         ],
@@ -95,7 +99,10 @@
             pl.BlockSpec((min(OUT_BLOCK, width), width), lambda j: (j, 0)),
         ],
         out_shape=[out, out],
-        scratch_shapes=[pltpu.VMEM((4, width, lanes), jnp.bfloat16)],
+        scratch_shapes=[
+            pltpu.VMEM((4, width, lanes), jnp.bfloat16),
+            pltpu.VMEM((3, ATOMS, lanes), jnp.bfloat16),
+        ],
         compiler_params=pltpu.CompilerParams(dimension_semantics=("arbitrary",)),
         cost_estimate=pl.CostEstimate(
             flops=2 * 2 * 3 * width * ATOMS * lanes + 4 * 2 * width * width * lanes,
@@ -118,10 +125,7 @@
 def shards(coordinates, resample, block_slot, lag_time, atom_pairs):
     chosen = gather_blocks(coordinates, resample, block_slot)
     width = F // lax.axis_size("row")
-    pairs = DRAWS * BLOCK_LEN
-    lanes = -(-pairs // 128) * 128
-    frames = jnp.transpose(chosen, (2, 3, 0, 1)).reshape(3, ATOMS, pairs)
-    frames = jnp.pad(frames, ((0, 0), (0, 0), (0, lanes - pairs)))
+    frames = jnp.transpose(chosen, (2, 3, 0, 1)).reshape(3, ATOMS, DRAWS * BLOCK_LEN)
     row_signed = signed_pairs(atom_pairs, lax.axis_index("row") * width, width)
     col_signed = signed_pairs(atom_pairs, lax.axis_index("col") * width, width)
     instant, crossed = covariances(lag_time, frames, row_signed, col_signed)

time: 74.1 us -> 74 us (level)
    pad x1 -> x0, local copies, waits for them, and re-layouts: 0.87 us -> none  [shards(): frames = jnp.pad(frames, ((0, 0), (0, 0), (0, lanes - pairs)))]
    reshape x1, local copies, waits for them, and re-layouts: 0.25 us -> 1.06 us  [shards(): jnp.transpose(chosen, (2, 3, 0, 1)).reshape(3, ATOMS, DRAWS * BLOCK_LEN)]
where the time goes in v9:
time: 74 us; the launch traced here: 72.8 us
  starting transfers between devices  23.5 us (32%)
  waiting for transfers between devices  21 us (28%)
  Pallas kernels  15.7 us (21%)
  local copies, waits for them, and re-layouts  7.08 us (10%)
  other arithmetic  4.2 us (6%)
  between operations  1.36 us (2%)
    all_to_all x1, starting transfers between devices, gather_blocks(): every = lax.all_to_all(spread, 'rep', 0, 0, tiled=True)  16.7 us
    pallas_call x1, Pallas kernels, covariances(): pl.pallas_call(covariance_kernel, grid=(pl.cdiv(width, OUT_BLOCK),), in_s...  15.7 us
    all_to_all x1, waiting for transfers between devices, gather_blocks(): every = lax.all_to_all(spread, 'rep', 0, 0, tiled=True)  14.4 us
    all_to_all x1, starting transfers between devices, gather_blocks(): parts = lax.all_to_all(spread, ('row', 'col'), 0, 0, tiled=True)  6.75 us
    all_to_all x1, waiting for transfers between devices, gather_blocks(): parts = lax.all_to_all(spread, ('row', 'col'), 0, 0, tiled=True)  6.59 us
    convert_element_type x2, other arithmetic, signed_pairs(): return ((first_atoms[:, None] == atom_ids).astype(jnp.float32) - (second_...  2.08 us
  transfers between devices with their start and end apart: 2, of which 2 were waited for; matrix products, arithmetic and copies ran while one was open for 9% of the time, Pallas kernels for 0%

profile of v9, /device:TPU:1, one launch (start us, length us, event | category | flops | bytes accessed | tf_op | source)
XLA Modules:
  0.0 72.8 jit_solution(8990658638935588876)
XLA Ops:
  0.6 0.0 copy-start
  0.7 0.9 %copy-done = bf16[4,32,3,128]{3,1,2,0:T(8,128)(2,1)S(1)} copy-done((bf16[4,32,3,128]{3,1,2,0:T(8,128)(2,1)S(1)}, bf16[4,32,3,128]{3,1,2,0:T(8,128)(2,1)}, u32[]{:S(2)}) %copy-start) | copy-done | bytes 98328
  1.5 0.8 %broadcast_in_dim.21 = bf16[32,4,2,3,128]{4,2,3,1,0:T(2,128)(2,1)} broadcast(bf16[4,2,3,128]{3,1,2,0:T(2,128)(2,1)S(1)} %constant_dynamic-slice_fusion.4), dimensions={1,2,3,4} | broadcast | bytes 202752 | tf_op jit(solution)/shard_map/broadcast_in_dim | solution.py:27
  2.3 16.7 %all-to-all-start = ((bf16[32,4,2,3,128]{4,2,3,1,0:T(2,128)(2,1)}), bf16[32,4,2,3,128]{4,2,3,1,0:T(2,128)(2,1)S(1)}, u32[]{:S(2)}, u32[]{:S(2)}) async-start(bf16[32,4,2,3,128]{4,2,3,1,0:T(2,128)(2,1)} %broadcast_in_dim.21), calls=%async_computation | async-start | bytes 393216 | tf_op jit(solution)/shard_map/all_to_all | solution.py:28
  19.1 0.7 fusion.1
  19.8 1.4 %gather_fusion = s32[22]{0:T(128)S(1)} fusion(s32[128]{0:T(128)} %param.7, s32[1024]{0:T(1024)S(1)} %pad_clamp_fusion.1), kind=kCustom, calls=%fused_computation | custom fusion | bytes 264 | tf_op jit(solution)/shard_map/jit(_take)/gather | solution.py:30
  21.1 0.7 compare_and_fusion
  21.8 0.7 fusion
  22.5 0.9 %fusion.2 = (s32[1,4096]{1,0:T(1,128)S(1)}, s32[1,4096]{1,0:T(1,128)S(1)}) fusion(s32[2,4096]{1,0:T(2,128)} %param.9), kind=kLoop, calls=%fused_computation.25 | loop fusion | bytes 65536 | tf_op jit(solution)/shard_map/slice | solution.py:116
  23.3 14.4 %all-to-all-done = bf16[32,4,2,3,128]{4,2,3,1,0:T(2,128)(2,1)S(1)} async-done(((bf16[32,4,2,3,128]{4,2,3,1,0:T(2,128)(2,1)}), bf16[32,4,2,3,128]{4,2,3,1,0:T(2,128)(2,1)S(1)}, u32[]{:S(2)}, u32[]{:S(2)}) %all-to-all-start) | async-done | bytes 196640 | tf_op jit(solution)/shard_map/all_to_all | solution.py:28
  37.7 0.6 gather_fusion.1
  38.3 0.1 broadcast_select_fusion
  38.4 1.1 %broadcast_in_dim.23 = bf16[16,22,2,3,128]{4,2,3,1,0:T(2,128)(2,1)} broadcast(bf16[22,2,3,128]{3,1,2,0:T(2,128)(2,1)S(1)} %broadcast_select_fusion), dimensions={1,2,3,4} | broadcast | bytes 574464 | tf_op jit(solution)/shard_map/broadcast_in_dim | solution.py:34
  39.5 6.8 %all-to-all-start.1 = ((bf16[16,22,2,3,128]{4,2,3,1,0:T(2,128)(2,1)}), bf16[16,22,2,3,128]{4,2,3,1,0:T(2,128)(2,1)S(1)}, u32[]{:S(2)}, u32[]{:S(2)}) async-start(bf16[16,22,2,3,128]{4,2,3,1,0:T(2,128)(2,1)} %broadcast_in_dim.23), calls=%async_computation.1 | async-start | bytes 1081344 | tf_op jit(solution)/shard_map/all_to_all | solution.py:35
  47.0 1.0 %subtract_convert_fusion.1.sr_ref = bf16[1024,128]{1,0:T(8,128)(2,1)} fusion(s32[1024]{0:T(1024)S(1)} %bitcast.36, s32[1024]{0:T(1024)S(1)} %bitcast.37), kind=kLoop, calls=%fused_computation.5 | loop fusion | flops 786432 | bytes 270336 | tf_op jit(solution)/shard_map/convert_element_type | solution.py:122
  48.0 1.0 %subtract_convert_fusion.sc_ref = bf16[1024,128]{1,0:T(8,128)(2,1)} fusion(s32[1024]{0:T(1024)S(1)} %bitcast.34, s32[1024]{0:T(1024)S(1)} %bitcast.35), kind=kLoop, calls=%fused_computation.2 | loop fusion | flops 786432 | bytes 270336 | tf_op jit(solution)/shard_map/convert_element_type | solution.py:122
  49.0 6.6 %all-to-all-done.1 = bf16[16,22,2,3,128]{4,2,3,1,0:T(2,128)(2,1)S(1)} async-done(((bf16[16,22,2,3,128]{4,2,3,1,0:T(2,128)(2,1)}), bf16[16,22,2,3,128]{4,2,3,1,0:T(2,128)(2,1)S(1)}, u32[]{:S(2)}, u32[]{:S(2)}) %all-to-all-start.1) | async-done | bytes 540704 | tf_op jit(solution)/shard_map/all_to_all | solution.py:35
  55.6 0.4 copy.10
  56.1 1.1 %copy.12.raw_ref = bf16[3,128,704]{2,1,0:T(8,128)(2,1)} copy(bf16[3,128,704]{1,2,0:T(8,128)(2,1)S(1)} %bitcast.32) | data formatting | bytes 1081344 | tf_op jit(solution)/shard_map/reshape | solution.py:128
  57.1 15.7 %shard_map.68 = (bf16[1024,1024]{1,0:T(8,128)(2,1)}, bf16[1024,1024]{1,0:T(8,128)(2,1)}) custom-call(s32[1]{0:T(128)S(6)} %copy.13.lag_ref, bf16[3,128,704]{2,1,0:T(8,128)(2,1)} %copy.12.raw_ref, bf16[1024,128]{1,0:T(8,128)(2,1)} %subtract_convert_fusion.1.sr_ref, bf16[1024,128]{1,0:T(8,128)(2,1)} %subtract_convert_fusion.sc_ref), custom_call_target="tpu_custom_call" | custom-call | flops 7650410496 | bytes 5308416 | tf_op jit(solution)/shard_map/pallas_call | solution.py:88
  (5 shorter events, 0.1 us)
Async XLA Ops:
  0.6 0.9 %copy-start = (bf16[4,32,3,128]{3,1,2,0:T(8,128)(2,1)S(1)}, bf16[4,32,3,128]{3,1,2,0:T(8,128)(2,1)}, u32[]{:S(2)}) copy-start(bf16[4,32,3,128]{3,1,2,0:T(8,128)(2,1)} %param.5) | copy-start | bytes 294916
  2.3 35.4 %all-to-all-start = ((bf16[32,4,2,3,128]{4,2,3,1,0:T(2,128)(2,1)}), bf16[32,4,2,3,128]{4,2,3,1,0:T(2,128)(2,1)S(1)}, u32[]{:S(2)}, u32[]{:S(2)}) async-start(bf16[32,4,2,3,128]{4,2,3,1,0:T(2,128)(2,1)} %broadcast_in_dim.21), calls=%async_computation | async-start | bytes 393216 | tf_op jit(solution)/shard_map/all_to_all | solution.py:28
  39.5 16.1 %all-to-all-start.1 = ((bf16[16,22,2,3,128]{4,2,3,1,0:T(2,128)(2,1)}), bf16[16,22,2,3,128]{4,2,3,1,0:T(2,128)(2,1)S(1)}, u32[]{:S(2)}, u32[]{:S(2)}) async-start(bf16[16,22,2,3,128]{4,2,3,1,0:T(2,128)(2,1)} %broadcast_in_dim.23), calls=%async_computation.1 | async-start | bytes 1081344 | tf_op jit(solution)/shard_map/all_to_all | solution.py:35

commit v10 on v7

--- a/solution.py
+++ b/solution.py
@@ -22,11 +22,11 @@
     member = lax.axis_index("row") * lax.axis_size("col") + lax.axis_index("col")
     if groups == 1:
         member = 0
-    piece = lax.dynamic_slice_in_dim(coordinates, member * frames, frames, axis=1)
-    reps = lax.axis_size("rep")
-    spread = jnp.broadcast_to(piece[None], (reps,) + piece.shape)
-    every = lax.all_to_all(spread, "rep", 0, 0, tiled=True)
-    every = every.reshape((-1,) + piece.shape[1:])
+    flat = coordinates.reshape(coordinates.shape[0], BLOCK_LEN, 3 * ATOMS)
+    piece = lax.dynamic_slice_in_dim(flat, member * frames, frames, axis=1)
+    piece = piece.reshape(piece.shape[0], -1)
+    every = lax.all_gather(piece, "rep", axis=0, tiled=True)
+    every = every.reshape(-1, frames, 3, ATOMS)
     slots = jnp.take(block_slot, resample[0], axis=0)
     picked = jnp.take(every, slots, axis=0)
     if groups == 1:

time: 74.1 us -> 79 us (1.066); the launches traced: 72.9 us -> 78.7 us
  blocking collectives: 0 us -> 38.1 us
  starting transfers between devices: 23.5 us -> 6.75 us
  waiting for transfers between devices: 21 us -> 7.53 us
  local copies, waits for them, and re-layouts: 7.13 us -> 4.95 us
    all_gather x0 -> x1, blocking collectives: none -> 38.1 us  [gather_blocks(): every = lax.all_gather(piece, 'rep', axis=0, tiled=True)]
    all_to_all x1 -> x0, starting transfers between devices: 16.7 us -> none  [gather_blocks(): every = lax.all_to_all(spread, 'rep', 0, 0, tiled=True)]
    all_to_all x1 -> x0, waiting for transfers between devices: 14.4 us -> none  [gather_blocks(): every = lax.all_to_all(spread, 'rep', 0, 0, tiled=True)]
    all_to_all x1, waiting for transfers between devices: 6.59 us -> 7.53 us  [gather_blocks(): parts = lax.all_to_all(spread, ('row', 'col'), 0, 0, tiled=True)]
    unnamed x2 -> x5, local copies, waits for them, and re-layouts: 0.88 us -> 0.03 us
    slice x1, local copies, waits for them, and re-layouts: 0.86 us -> 0.03 us  [signed_pairs(): first_atoms = lax.dynamic_slice_in_dim(atom_pairs[0], first_feature, width)]
  transfers between devices with their start and end apart: 2 -> 1, of which waited for: 2 -> 1; matrix products, arithmetic and copies ran while one was open for 9% -> 3% of each run, Pallas kernels for 0% -> 0%
where the time goes in v10:
time: 79 us; the launch traced here: 78.7 us
  blocking collectives  38.1 us (48%)
  Pallas kernels  15.7 us (20%)
  waiting for transfers between devices  7.53 us (10%)
  starting transfers between devices  6.75 us (9%)
  local copies, waits for them, and re-layouts  4.95 us (6%)
  other arithmetic  4.22 us (5%)
  between operations  1.4 us (2%)
    all_gather x1, blocking collectives, gather_blocks(): every = lax.all_gather(piece, 'rep', axis=0, tiled=True)  38.1 us
    pallas_call x1, Pallas kernels, covariances(): pl.pallas_call(covariance_kernel, grid=(pl.cdiv(width, OUT_BLOCK),), in_s...  15.7 us
    all_to_all x1, waiting for transfers between devices, gather_blocks(): parts = lax.all_to_all(spread, ('row', 'col'), 0, 0, tiled=True)  7.53 us
    all_to_all x1, starting transfers between devices, gather_blocks(): parts = lax.all_to_all(spread, ('row', 'col'), 0, 0, tiled=True)  6.75 us
    convert_element_type x2, other arithmetic, signed_pairs(): return ((first_atoms[:, None] == atom_ids).astype(jnp.float32) - (second_...  2.07 us
  transfers between devices with their start and end apart: 1, of which 1 were waited for; matrix products, arithmetic and copies ran while one was open for 3% of the time, Pallas kernels for 0%

profile of v10, /device:TPU:1, one launch (start us, length us, event | category | flops | bytes accessed | tf_op | source)
XLA Modules:
  0.0 78.7 jit_solution(16580796302924729255)
XLA Ops:
  0.6 0.0 copy-start
  0.6 0.0 copy-start.1
  0.7 0.7 fusion.1
  1.4 1.4 %gather_fusion = s32[22]{0:T(128)S(1)} fusion(s32[128]{0:T(128)} %param.7, s32[1024]{0:T(1024)S(1)} %pad_clamp_fusion.1), kind=kCustom, calls=%fused_computation | custom fusion | bytes 264 | tf_op jit(solution)/shard_map/jit(_take)/gather | solution.py:30
  2.7 0.7 compare_and_fusion
  3.4 0.7 fusion
  4.1 0.0 copy-done
  4.1 38.1 %all-gather = bf16[32,4,768]{2,1,0:T(4,128)(2,1)S(1)} all-gather(bf16[1,4,768]{2,1,0:T(4,128)(2,1)S(1)} %reshape.131), channel_id=1, replica_groups=mesh['rep'=32,'row'=4,'col'=4] {'rep'}, dimensions={0}, use_global_device_ids=true | all-gather | bytes 202752 | tf_op jit(solution)/shard_map/all_gather | solution.py:28
  42.2 0.1 reshape.112
  42.3 0.2 copy.12
  42.5 0.6 gather_fusion.1
  43.1 0.1 broadcast_select_fusion
  43.3 1.1 %broadcast_in_dim.32 = bf16[16,22,2,3,128]{4,2,3,1,0:T(2,128)(2,1)} broadcast(bf16[22,2,3,128]{3,1,2,0:T(2,128)(2,1)S(1)} %broadcast_select_fusion), dimensions={1,2,3,4} | broadcast | bytes 574464 | tf_op jit(solution)/shard_map/broadcast_in_dim | solution.py:34
  44.3 6.8 %all-to-all-start = ((bf16[16,22,2,3,128]{4,2,3,1,0:T(2,128)(2,1)}), bf16[16,22,2,3,128]{4,2,3,1,0:T(2,128)(2,1)S(1)}, u32[]{:S(2)}, u32[]{:S(2)}) async-start(bf16[16,22,2,3,128]{4,2,3,1,0:T(2,128)(2,1)} %broadcast_in_dim.32), calls=%async_computation | async-start | bytes 1081344 | tf_op jit(solution)/shard_map/all_to_all | solution.py:35
  51.1 0.0 copy-done.1
  51.8 1.0 %subtract_convert_fusion.1.sr_ref = bf16[1024,128]{1,0:T(8,128)(2,1)} fusion(s32[1024]{0:T(1024)S(1)} %bitcast.39, s32[1024]{0:T(1024)S(1)} %bitcast.40), kind=kLoop, calls=%fused_computation.5 | loop fusion | flops 786432 | bytes 270336 | tf_op jit(solution)/shard_map/convert_element_type | solution.py:115
  52.9 1.0 %subtract_convert_fusion.sc_ref = bf16[1024,128]{1,0:T(8,128)(2,1)} fusion(s32[1024]{0:T(1024)S(1)} %bitcast.37, s32[1024]{0:T(1024)S(1)} %bitcast.38), kind=kLoop, calls=%fused_computation.2 | loop fusion | flops 786432 | bytes 270336 | tf_op jit(solution)/shard_map/convert_element_type | solution.py:115
  53.9 7.5 %all-to-all-done = bf16[16,22,2,3,128]{4,2,3,1,0:T(2,128)(2,1)S(1)} async-done(((bf16[16,22,2,3,128]{4,2,3,1,0:T(2,128)(2,1)}), bf16[16,22,2,3,128]{4,2,3,1,0:T(2,128)(2,1)S(1)}, u32[]{:S(2)}, u32[]{:S(2)}) %all-to-all-start) | async-done | bytes 540704 | tf_op jit(solution)/shard_map/all_to_all | solution.py:35
  61.4 0.4 copy.13
  61.8 0.2 copy.15
  62.1 0.9 %pad.4.x_ref = bf16[3,128,768]{2,1,0:T(8,128)(2,1)} pad(bf16[3,128,704]{2,1,0:T(8,128)(2,1)S(1)} %copy.15, bf16[]{:T(256)} %constant.50.clone.1), padding=0_0x0_0x0_64 | pad | bytes 1130498 | tf_op jit(solution)/shard_map/jit(_pad)/pad | solution.py:124
  63.0 15.7 %shard_map.68 = (bf16[1024,1024]{1,0:T(8,128)(2,1)}, bf16[1024,1024]{1,0:T(8,128)(2,1)}) custom-call(s32[1]{0:T(128)S(6)} %copy.18.lag_ref, bf16[3,128,768]{2,1,0:T(8,128)(2,1)} %pad.4.x_ref, bf16[1024,128]{1,0:T(8,128)(2,1)} %subtract_convert_fusion.1.sr_ref, bf16[1024,128]{1,0:T(8,128)(2,1)} %subtract_convert_fusion.sc_ref), custom_call_target="tpu_custom_call" | custom-call | flops 7650410496 | bytes 5308416 | tf_op jit(solution)/shard_map/pallas_call | solution.py:84
  (8 shorter events, 0.1 us)
Async XLA Ops:
  0.6 3.4 %copy-start = (bf16[4,32,3,128]{3,1,2,0:T(8,128)(2,1)S(1)}, bf16[4,32,3,128]{3,1,2,0:T(8,128)(2,1)}, u32[]{:S(2)}) copy-start(bf16[4,32,3,128]{3,1,2,0:T(8,128)(2,1)} %param.5) | copy-start | bytes 294916
  0.6 50.5 %copy-start.1 = (s32[2,4096]{1,0:T(2,128)S(1)}, s32[2,4096]{1,0:T(2,128)}, u32[]{:S(2)}) copy-start(s32[2,4096]{1,0:T(2,128)} %param.9) | copy-start | bytes 98308
  44.3 17.1 %all-to-all-start = ((bf16[16,22,2,3,128]{4,2,3,1,0:T(2,128)(2,1)}), bf16[16,22,2,3,128]{4,2,3,1,0:T(2,128)(2,1)S(1)}, u32[]{:S(2)}, u32[]{:S(2)}) async-start(bf16[16,22,2,3,128]{4,2,3,1,0:T(2,128)(2,1)} %broadcast_in_dim.32), calls=%async_computation | async-start | bytes 1081344 | tf_op jit(solution)/shard_map/all_to_all | solution.py:35

commit v11 on v7

--- a/solution.py
+++ b/solution.py
@@ -59,21 +59,21 @@
             mean = (
                 jnp.sum(earlier, axis=1, keepdims=True) + jnp.sum(later, axis=1, keepdims=True)
             ) / count
-            stack_ref[2 * tile] = jnp.where(first, earlier - mean, 0.0).astype(jnp.bfloat16)
-            stack_ref[2 * tile + 1] = jnp.where(first, later - mean, 0.0).astype(jnp.bfloat16)
+            zero_lag = jnp.where(first, earlier - mean, 0.0).astype(jnp.bfloat16)
+            lagged = jnp.where(first, later - mean, 0.0).astype(jnp.bfloat16)
+            stack_ref[tile, :, :lanes] = zero_lag
+            stack_ref[tile, :, lanes:] = lagged
+            if tile == 1:
+                stack_ref[2, :, :lanes] = lagged
+                stack_ref[2, :, lanes:] = zero_lag
 
     block = inst_ref.shape[0]
     rows = pl.ds(pl.multiple_of(pl.program_id(0) * block, block), block)
     nt = (((1,), (1,)), ((), ()))
-    zero_row = stack_ref[0, rows, :]
-    lag_row = stack_ref[1, rows, :]
-    zero_col = stack_ref[2]
-    lag_col = stack_ref[3]
-    instant = lax.dot_general(zero_row, zero_col, nt, preferred_element_type=jnp.float32)
-    instant = instant + lax.dot_general(lag_row, lag_col, nt, preferred_element_type=jnp.float32)
+    stacked = stack_ref[0, rows, :]
+    instant = lax.dot_general(stacked, stack_ref[1], nt, preferred_element_type=jnp.float32)
     inst_ref[...] = (instant / count).astype(inst_ref.dtype)
-    crossed = lax.dot_general(zero_row, lag_col, nt, preferred_element_type=jnp.float32)
-    crossed = crossed + lax.dot_general(lag_row, zero_col, nt, preferred_element_type=jnp.float32)
+    crossed = lax.dot_general(stacked, stack_ref[2], nt, preferred_element_type=jnp.float32)
     cross_ref[...] = (crossed / count).astype(cross_ref.dtype)
 
 
@@ -95,7 +95,7 @@
             pl.BlockSpec((min(OUT_BLOCK, width), width), lambda j: (j, 0)),
         ],
         out_shape=[out, out],
-        scratch_shapes=[pltpu.VMEM((4, width, lanes), jnp.bfloat16)],
+        scratch_shapes=[pltpu.VMEM((3, width, 2 * lanes), jnp.bfloat16)],
         compiler_params=pltpu.CompilerParams(dimension_semantics=("arbitrary",)),
         cost_estimate=pl.CostEstimate(
             flops=2 * 2 * 3 * width * ATOMS * lanes + 4 * 2 * width * width * lanes,

time: 74.1 us -> 74 us (level)
  no operation moved by 1% of the time
where the time goes in v11:
time: 74 us; the launch traced here: 72.8 us
  starting transfers between devices  23.5 us (32%)
  waiting for transfers between devices  21 us (28%)
  Pallas kernels  15.6 us (21%)
  local copies, waits for them, and re-layouts  7.14 us (10%)
  other arithmetic  4.2 us (6%)
  between operations  1.36 us (2%)
    all_to_all x1, starting transfers between devices, gather_blocks(): every = lax.all_to_all(spread, 'rep', 0, 0, tiled=True)  16.7 us
    pallas_call x1, Pallas kernels, covariances(): pl.pallas_call(covariance_kernel, grid=(pl.cdiv(width, OUT_BLOCK),), in_s...  15.6 us
    all_to_all x1, waiting for transfers between devices, gather_blocks(): every = lax.all_to_all(spread, 'rep', 0, 0, tiled=True)  14.4 us
    all_to_all x1, starting transfers between devices, gather_blocks(): parts = lax.all_to_all(spread, ('row', 'col'), 0, 0, tiled=True)  6.75 us
    all_to_all x1, waiting for transfers between devices, gather_blocks(): parts = lax.all_to_all(spread, ('row', 'col'), 0, 0, tiled=True)  6.59 us
    convert_element_type x2, other arithmetic, signed_pairs(): return ((first_atoms[:, None] == atom_ids).astype(jnp.float32) - (second_...  2.08 us
  transfers between devices with their start and end apart: 2, of which 2 were waited for; matrix products, arithmetic and copies ran while one was open for 9% of the time, Pallas kernels for 0%

profile of v11, /device:TPU:1, one launch (start us, length us, event | category | flops | bytes accessed | tf_op | source)
XLA Modules:
  0.0 72.8 jit_solution(16648177022835400288)
XLA Ops:
  0.6 0.0 copy-start
  0.7 0.9 %copy-done = bf16[4,32,3,128]{3,1,2,0:T(8,128)(2,1)S(1)} copy-done((bf16[4,32,3,128]{3,1,2,0:T(8,128)(2,1)S(1)}, bf16[4,32,3,128]{3,1,2,0:T(8,128)(2,1)}, u32[]{:S(2)}) %copy-start) | copy-done | bytes 98328
  1.5 0.8 %broadcast_in_dim.21 = bf16[32,4,2,3,128]{4,2,3,1,0:T(2,128)(2,1)} broadcast(bf16[4,2,3,128]{3,1,2,0:T(2,128)(2,1)S(1)} %constant_dynamic-slice_fusion.4), dimensions={1,2,3,4} | broadcast | bytes 202752 | tf_op jit(solution)/shard_map/broadcast_in_dim | solution.py:27
  2.3 16.7 %all-to-all-start = ((bf16[32,4,2,3,128]{4,2,3,1,0:T(2,128)(2,1)}), bf16[32,4,2,3,128]{4,2,3,1,0:T(2,128)(2,1)S(1)}, u32[]{:S(2)}, u32[]{:S(2)}) async-start(bf16[32,4,2,3,128]{4,2,3,1,0:T(2,128)(2,1)} %broadcast_in_dim.21), calls=%async_computation | async-start | bytes 393216 | tf_op jit(solution)/shard_map/all_to_all | solution.py:28
  19.1 0.7 fusion.1
  19.8 1.4 %gather_fusion = s32[22]{0:T(128)S(1)} fusion(s32[128]{0:T(128)} %param.7, s32[1024]{0:T(1024)S(1)} %pad_clamp_fusion.1), kind=kCustom, calls=%fused_computation | custom fusion | bytes 264 | tf_op jit(solution)/shard_map/jit(_take)/gather | solution.py:30
  21.1 0.7 compare_and_fusion
  21.8 0.7 fusion
  22.5 0.9 %fusion.2 = (s32[1,4096]{1,0:T(1,128)S(1)}, s32[1,4096]{1,0:T(1,128)S(1)}) fusion(s32[2,4096]{1,0:T(2,128)} %param.9), kind=kLoop, calls=%fused_computation.25 | loop fusion | bytes 65536 | tf_op jit(solution)/shard_map/slice | solution.py:109
  23.3 14.4 %all-to-all-done = bf16[32,4,2,3,128]{4,2,3,1,0:T(2,128)(2,1)S(1)} async-done(((bf16[32,4,2,3,128]{4,2,3,1,0:T(2,128)(2,1)}), bf16[32,4,2,3,128]{4,2,3,1,0:T(2,128)(2,1)S(1)}, u32[]{:S(2)}, u32[]{:S(2)}) %all-to-all-start) | async-done | bytes 196640 | tf_op jit(solution)/shard_map/all_to_all | solution.py:28
  37.7 0.6 gather_fusion.1
  38.3 0.1 broadcast_select_fusion
  38.4 1.1 %broadcast_in_dim.23 = bf16[16,22,2,3,128]{4,2,3,1,0:T(2,128)(2,1)} broadcast(bf16[22,2,3,128]{3,1,2,0:T(2,128)(2,1)S(1)} %broadcast_select_fusion), dimensions={1,2,3,4} | broadcast | bytes 574464 | tf_op jit(solution)/shard_map/broadcast_in_dim | solution.py:34
  39.5 6.8 %all-to-all-start.1 = ((bf16[16,22,2,3,128]{4,2,3,1,0:T(2,128)(2,1)}), bf16[16,22,2,3,128]{4,2,3,1,0:T(2,128)(2,1)S(1)}, u32[]{:S(2)}, u32[]{:S(2)}) async-start(bf16[16,22,2,3,128]{4,2,3,1,0:T(2,128)(2,1)} %broadcast_in_dim.23), calls=%async_computation.1 | async-start | bytes 1081344 | tf_op jit(solution)/shard_map/all_to_all | solution.py:35
  47.0 1.0 %subtract_convert_fusion.1.sr_ref = bf16[1024,128]{1,0:T(8,128)(2,1)} fusion(s32[1024]{0:T(1024)S(1)} %bitcast.36, s32[1024]{0:T(1024)S(1)} %bitcast.37), kind=kLoop, calls=%fused_computation.5 | loop fusion | flops 786432 | bytes 270336 | tf_op jit(solution)/shard_map/convert_element_type | solution.py:115
  48.0 1.0 %subtract_convert_fusion.sc_ref = bf16[1024,128]{1,0:T(8,128)(2,1)} fusion(s32[1024]{0:T(1024)S(1)} %bitcast.34, s32[1024]{0:T(1024)S(1)} %bitcast.35), kind=kLoop, calls=%fused_computation.2 | loop fusion | flops 786432 | bytes 270336 | tf_op jit(solution)/shard_map/convert_element_type | solution.py:115
  49.0 6.6 %all-to-all-done.1 = bf16[16,22,2,3,128]{4,2,3,1,0:T(2,128)(2,1)S(1)} async-done(((bf16[16,22,2,3,128]{4,2,3,1,0:T(2,128)(2,1)}), bf16[16,22,2,3,128]{4,2,3,1,0:T(2,128)(2,1)S(1)}, u32[]{:S(2)}, u32[]{:S(2)}) %all-to-all-start.1) | async-done | bytes 540704 | tf_op jit(solution)/shard_map/all_to_all | solution.py:35
  55.6 0.4 copy.10
  56.1 0.2 copy.12
  56.3 0.9 %pad.4.x_ref = bf16[3,128,768]{2,1,0:T(8,128)(2,1)} pad(bf16[3,128,704]{2,1,0:T(8,128)(2,1)S(1)} %copy.12, bf16[]{:T(256)} %constant.50.clone.1), padding=0_0x0_0x0_64 | pad | bytes 1130498 | tf_op jit(solution)/shard_map/jit(_pad)/pad | solution.py:124
  57.2 15.6 %shard_map.68 = (bf16[1024,1024]{1,0:T(8,128)(2,1)}, bf16[1024,1024]{1,0:T(8,128)(2,1)}) custom-call(s32[1]{0:T(128)S(6)} %copy.13.lag_ref, bf16[3,128,768]{2,1,0:T(8,128)(2,1)} %pad.4.x_ref, bf16[1024,128]{1,0:T(8,128)(2,1)} %subtract_convert_fusion.1.sr_ref, bf16[1024,128]{1,0:T(8,128)(2,1)} %subtract_convert_fusion.sc_ref), custom_call_target="tpu_custom_call" | custom-call | flops 7650410496 | bytes 5308416 | tf_op jit(solution)/shard_map/pallas_call | solution.py:84
  (5 shorter events, 0.1 us)
Async XLA Ops:
  0.6 0.9 %copy-start = (bf16[4,32,3,128]{3,1,2,0:T(8,128)(2,1)S(1)}, bf16[4,32,3,128]{3,1,2,0:T(8,128)(2,1)}, u32[]{:S(2)}) copy-start(bf16[4,32,3,128]{3,1,2,0:T(8,128)(2,1)} %param.5) | copy-start | bytes 294916
  2.3 35.4 %all-to-all-start = ((bf16[32,4,2,3,128]{4,2,3,1,0:T(2,128)(2,1)}), bf16[32,4,2,3,128]{4,2,3,1,0:T(2,128)(2,1)S(1)}, u32[]{:S(2)}, u32[]{:S(2)}) async-start(bf16[32,4,2,3,128]{4,2,3,1,0:T(2,128)(2,1)} %broadcast_in_dim.21), calls=%async_computation | async-start | bytes 393216 | tf_op jit(solution)/shard_map/all_to_all | solution.py:28
  39.5 16.1 %all-to-all-start.1 = ((bf16[16,22,2,3,128]{4,2,3,1,0:T(2,128)(2,1)}), bf16[16,22,2,3,128]{4,2,3,1,0:T(2,128)(2,1)S(1)}, u32[]{:S(2)}, u32[]{:S(2)}) async-start(bf16[16,22,2,3,128]{4,2,3,1,0:T(2,128)(2,1)} %broadcast_in_dim.23), calls=%async_computation.1 | async-start | bytes 1081344 | tf_op jit(solution)/shard_map/all_to_all | solution.py:35
